TPU v7x, 32 devices: a whole 2x2x4 slice. The times are simulated.
32 devices in a mesh: clips: 2 (over y), frames: 4 (over z), wshard: 4 (over x, core).
Axes of the slice: x: 2, y: 2, z: 4, core: 2. Of those that a mesh axis runs over, the one named last changes fastest.
Arguments:
- tokens: bfloat16 [6144, 5120], P(('clips', 'frames')), parts along dimension 0, may hold values from -17 to 17
- w_query: bfloat16 [5120, 3072], P('frames', 'wshard'), may hold values from -0.08385255 to 0.08385255
- w_key: bfloat16 [5120, 3072], P('frames', 'wshard'), may hold values from -0.08385255 to 0.08385255
- w_value: bfloat16 [5120, 3072], P('frames', 'wshard'), may hold values from -0.078125 to 0.078125
- q_gain: float32 [3072], P('wshard'), may hold values from 0.4 to 7
- k_gain: float32 [3072], P('wshard'), may hold values from 0.4 to 7
- w_out: bfloat16 [3072, 5120], P('frames', 'wshard'), may hold values from -0.109375 to 0.109375
- key_blocks: int32 [48, 8], P(('clips', 'frames')), parts along dimension 0, may hold values from 0 to 17, as said below
- slab_counts: int32 [8], P('clips'), parts along dimension 0, may hold values from 384 to 768, as said below
Outputs:
- mixed: bfloat16 [6144, 5120], P(('clips', 'frames'), 'wshard'), parts along dimension 0
There are 2 independent parts, one for each index of `clips`. A program takes and returns all parts, laid end to end along the dimension named above; an argument that names none is the same for every part. Nothing has to cross between parts.
Inputs may be any that keep to these rules, and one draw needn't show every extreme that they name: `key_blocks`: each row names 8 different blocks of its window, among them the query's own block, number 6 + i for block i of a slab. `slab_counts`: some slab is full in every clip.
All inputs are finite; a program needn't handle non-finite values.
Results may differ from a plain program's by a relative error of at most 0.0085.
Values may be sent and summed in bfloat16 or wider, within the bound.
No kernel may reach another device: no remote copies, remote signals or barrier semaphores. Data moves between devices by JAX's collectives and lax.ppermute only.
A program may use at most 192 MiB of HBM per device.

v0:
```python
import functools
import math

import jax
import jax.numpy as jnp
from jax import lax
from jax.experimental import pallas as pl
from jax.experimental.pallas import tpu as pltpu
from jax.sharding import PartitionSpec as P


HEAD_DIM = 128
TILE = 128


def shifted(value, axis, by):
    size = lax.axis_size(axis)
    pairs = [(i, i + by) for i in range(size) if 0 <= i + by < size]
    return lax.ppermute(value, axis, pairs)


def head_norm(raw, gain):
    rows, cols = raw.shape
    split = raw.reshape(rows, cols // HEAD_DIM, HEAD_DIM)
    square = jnp.mean(split * split, axis=-1, keepdims=True)
    normed = (split * lax.rsqrt(square + 1e-06)).reshape(rows, cols)
    return (normed * gain).astype(jnp.bfloat16)


def attend_kernel(kb_ref, lim_ref, q_ref, k_ref, v_ref, o_ref, *, first_tile):
    tiles = q_ref.shape[0] // TILE
    slab_tiles = k_ref.shape[0] // (3 * TILE)
    picks = kb_ref.shape[1]
    scale = 1.0 / math.sqrt(HEAD_DIM)
    lanes = lax.broadcasted_iota(jnp.int32, (1, TILE), 1)
    rows = lax.broadcasted_iota(jnp.int32, (TILE, 1), 0)

    def one_tile(i, carry):
        start = pl.multiple_of(i * TILE, TILE)
        q = q_ref[pl.ds(start, TILE), :]
        scores = []
        for j in range(picks):
            b = kb_ref[i, j]
            k = k_ref[pl.ds(pl.multiple_of(b * TILE, TILE), TILE), :]
            s = lax.dot_general(
                q, k, (((1,), (1,)), ((), ())), preferred_element_type=jnp.float32
            )
            slab = (b >= slab_tiles).astype(jnp.int32) + (b >= 2 * slab_tiles).astype(jnp.int32)
            limit = lim_ref[slab]
            pos = (b - slab * slab_tiles) * TILE + lanes
            scores.append(jnp.where(pos < limit, s, -1e30))
        top = scores[0]
        for s in scores[1:]:
            top = jnp.maximum(top, s)
        top = jnp.max(top, axis=1, keepdims=True)
        expo = [jnp.exp((s - top) * scale) for s in scores]
        total = expo[0]
        for e in expo[1:]:
            total = total + e
        total = jnp.sum(total, axis=1, keepdims=True)
        acc = None
        for j in range(picks):
            b = kb_ref[i, j]
            v = v_ref[pl.ds(pl.multiple_of(b * TILE, TILE), TILE), :]
            w = (expo[j] / total).astype(jnp.bfloat16)
            part = jnp.dot(w, v, preferred_element_type=jnp.float32)
            acc = part if acc is None else acc + part
        live = (i + first_tile) * TILE + rows < lim_ref[1]
        o_ref[pl.ds(start, TILE), :] = jnp.where(live, acc, 0.0).astype(o_ref.dtype)
        return carry

    lax.fori_loop(0, tiles, one_tile, 0)


def attend(query, keys, values, blocks, limits, first_tile=0, interpret=False):
    rows, cols = query.shape
    window = keys.shape[0]
    heads = cols // HEAD_DIM
    spec = pltpu.PrefetchScalarGridSpec(
        num_scalar_prefetch=2,
        grid=(heads,),
        in_specs=[
            pl.BlockSpec((rows, HEAD_DIM), lambda h, kb, lim: (0, h)),
            pl.BlockSpec((window, HEAD_DIM), lambda h, kb, lim: (0, h)),
            pl.BlockSpec((window, HEAD_DIM), lambda h, kb, lim: (0, h)),
        ],
        out_specs=pl.BlockSpec((rows, HEAD_DIM), lambda h, kb, lim: (0, h)),
    )
    return pl.pallas_call(
        functools.partial(attend_kernel, first_tile=first_tile),
        grid_spec=spec,
        out_shape=jax.ShapeDtypeStruct((rows, cols), jnp.bfloat16),
        interpret=interpret,
    )(blocks.astype(jnp.int32), limits.astype(jnp.int32), query, keys, values)


def fetch(piece):
    assert lax.axis_size("clips") == 2
    ci = lax.axis_index("clips")
    share = piece.shape[1] // 2
    mine = lax.dynamic_slice_in_dim(piece, ci * share, share, 1)
    other = lax.dynamic_slice_in_dim(piece, (1 - ci) * share, share, 1)
    return lax.all_gather(mine, "frames", axis=0, tiled=True), other


def trade(fetched):
    got, other = fetched
    rows = other.shape[0]
    chunks = got.shape[0] // rows
    fi = lax.axis_index("frames")
    recv = []
    for k in range(1, chunks):
        at = (fi + k) % chunks
        part = lax.dynamic_slice_in_dim(got, at * rows, rows, 0)
        recv.append(lax.ppermute(part, "clips", [(0, 1), (1, 0)]))
    return got, other, recv


def split_dot(x, traded):
    got, other, recv = traded
    rows = other.shape[0]
    chunks = got.shape[0] // rows
    fi = lax.axis_index("frames")
    own = jnp.dot(x, got, preferred_element_type=jnp.float32)
    rest = jnp.dot(lax.dynamic_slice_in_dim(x, fi * rows, rows, 1), other,
                   preferred_element_type=jnp.float32)
    for k, part in enumerate(recv, 1):
        at = (fi + k) % chunks
        rest = rest + jnp.dot(lax.dynamic_slice_in_dim(x, at * rows, rows, 1), part,
                              preferred_element_type=jnp.float32)
    first = lax.axis_index("clips") == 0
    return jnp.where(first, jnp.concatenate([own, rest], 1), jnp.concatenate([rest, own], 1))


def layer(tokens, w_query, w_key, w_value, q_gain, k_gain, w_out, key_blocks, slab_counts):
    k_got = fetch(w_key)
    v_got = fetch(w_value)
    q_got = fetch(w_query)
    o_got = fetch(w_out)
    keys = head_norm(split_dot(tokens, trade(k_got)), k_gain)
    values = split_dot(tokens, trade(v_got)).astype(jnp.bfloat16)
    keys, values, q_got = lax.optimization_barrier((keys, values, q_got))
    query = head_norm(split_dot(tokens, trade(q_got)), q_gain)
    keys, values, o_got = lax.optimization_barrier((keys, values, o_got))
    o_rows = trade(o_got)
    before = shifted((keys, values), "frames", 1)
    after = shifted((keys, values), "frames", -1)
    key_window = jnp.concatenate([before[0], keys, after[0]], axis=0)
    value_window = jnp.concatenate([before[1], values, after[1]], axis=0)
    position = lax.axis_index("frames")
    zero = jnp.zeros((1,), jnp.int32)
    count_pad = jnp.concatenate([zero, slab_counts, zero], axis=0)
    limits = lax.dynamic_slice_in_dim(count_pad, position, 3, 0)
    tiles = query.shape[0] // TILE
    half = tiles // 2
    mixed = []
    for lo, hi in ((0, half), (half, tiles)):
        part = attend(query[lo * TILE:hi * TILE], key_window, value_window,
                      key_blocks[lo:hi], limits, lo)
        whole = lax.all_gather(part, "wshard", axis=1, tiled=True)
        mixed.append(split_dot(whole, o_rows).astype(jnp.bfloat16))
    return jnp.concatenate(mixed, axis=0)


def solution(mesh):
    return jax.shard_map(
        layer,
        mesh=mesh,
        in_specs=(
            P(("clips", "frames"), None),
            P("frames", "wshard"),
            P("frames", "wshard"),
            P("frames", "wshard"),
            P("wshard"),
            P("wshard"),
            P("frames", "wshard"),
            P(("clips", "frames"), None),
            P("clips"),
        ),
        out_specs=P(("clips", "frames"), "wshard"),
        check_vma=False,
    )
```

profile of v0, /device:TPU:0, one launch (start us, length us, event | category | flops | bytes accessed | tf_op | source)
XLA Modules:
  0.0 513.0 jit_solution(3924170414868630995)
XLA Ops:
  6.5 2.5 constant_dynamic-slice_fusion.13
  10.2 3.0 constant_dynamic-slice_fusion.8
  13.3 3.0 constant_dynamic-slice_fusion.3
  16.4 3.7 fusion.25
  20.1 2.9 fusion.23
  24.3 64.1 %all-gather.9.cloned.1.call-done = bf16[5120,384]{1,0:T(8,128)(2,1)} async-done(((bf16[1280,384]{1,0:T(8,128)(2,1)}), bf16[5120,384]{1,0:T(8,128)(2,1)}) %all-gather.9.cloned.1.call-update) | async-done | bytes 3932176 | tf_op jit(solution)/shard_map/all_gather | solution.py:103
  88.3 3.5 constant_dynamic-slice_fusion.12
  91.8 1.5 collective-permute-start.3
  93.9 71.0 %all-gather.7.cloned.1.call-done = bf16[5120,384]{1,0:T(8,128)(2,1)} async-done(((bf16[1280,384]{1,0:T(8,128)(2,1)}), bf16[5120,384]{1,0:T(8,128)(2,1)}) %all-gather.7.cloned.1.call-update) | async-done | bytes 3932176 | tf_op jit(solution)/shard_map/all_gather | solution.py:103
  164.9 2.2 constant_dynamic-slice_fusion.16
  167.1 1.5 collective-permute-start
  169.2 1.5 collective-permute-start.1
  170.7 6.9 %fusion.94 = f32[384,768]{1,0:T(8,128)S(1)} fusion(bf16[5120,384]{1,0:T(8,128)(2,1)S(1)} %copy-done.11, bf16[768,5120]{1,0:T(8,128)(2,1)} %param.9), kind=kOutput, calls=%fused_computation.118 | convolution fusion | flops 3019898880 | bytes 12976128 | tf_op jit(solution)/shard_map/dot_general | solution.py:124
  177.7 5.0 convolution_bitcast_fusion
  182.7 30.2 %collective-permute-done.2 = bf16[1280,384]{1,0:T(8,128)(2,1)S(1)} collective-permute-done((bf16[1280,384]{1,0:T(8,128)(2,1)S(1)}, bf16[1280,384]{1,0:T(8,128)(2,1)S(1)}, u32[]{:S(2)}, u32[]{:S(2)}) %collective-permute-start.2) | collective-permute-done | bytes 983072 | tf_op jit(solution)/shard_map/ppermute | solution.py:115
  212.9 1.5 collective-permute-start.4
  215.4 18.6 %collective-permute-done.1 = bf16[1280,384]{1,0:T(8,128)(2,1)S(1)} collective-permute-done((bf16[1280,384]{1,0:T(8,128)(2,1)S(1)}, bf16[1280,384]{1,0:T(8,128)(2,1)S(1)}, u32[]{:S(2)}, u32[]{:S(2)}) %collective-permute-start.1) | collective-permute-done | bytes 983072 | tf_op jit(solution)/shard_map/ppermute | solution.py:115
  235.0 1.2 fusion.49
  236.7 2.0 copy.23
  238.7 3.0 fusion.5
  241.7 12.1 %collective-permute-done.4 = bf16[1280,384]{1,0:T(8,128)(2,1)} collective-permute-done((bf16[1280,384]{1,0:T(8,128)(2,1)}, bf16[1280,384]{1,0:T(8,128)(2,1)}, u32[]{:S(2)}, u32[]{:S(2)}) %collective-permute-start.4) | collective-permute-done | bytes 983072 | tf_op jit(solution)/shard_map/ppermute | solution.py:115
  253.8 3.0 fusion.11
  256.8 3.1 fusion.52
  260.0 1.4 fusion
  262.1 1.2 multiply_convert_fusion.1
  263.3 3.2 constant_dynamic-slice_fusion.7
  266.5 1.5 collective-permute-start.6
  268.5 1.5 collective-permute-start.7
  270.0 5.6 %fusion.95 = f32[384,768]{1,0:T(8,128)S(1)} fusion(bf16[5120,384]{1,0:T(8,128)(2,1)S(1)} %copy-done.9, bf16[768,5120]{1,0:T(8,128)(2,1)} %param.9), kind=kOutput, calls=%fused_computation.119 | convolution fusion | flops 3019898880 | bytes 12976128 | tf_op jit(solution)/shard_map/dot_general | solution.py:124
  275.7 42.2 %all-gather.13.cloned.1.call-done = bf16[3072,640]{1,0:T(8,128)(2,1)} async-done(((bf16[768,640]{1,0:T(8,128)(2,1)}), bf16[3072,640]{1,0:T(8,128)(2,1)}) %all-gather.13.cloned.1.call-update) | async-done | bytes 3932176 | tf_op jit(solution)/shard_map/all_gather | solution.py:103
  317.8 1.3 collective-permute-start.10
  319.1 5.6 %collective-permute-start.9 = (bf16[768,768]{1,0:T(8,128)(2,1)}, bf16[768,768]{1,0:T(8,128)(2,1)}, u32[]{:S(2)}, u32[]{:S(2)}) collective-permute-start(bf16[768,768]{1,0:T(8,128)(2,1)} %multiply_convert_fusion.1), channel_id=1, source_target_pairs={{0,4},{4,8},{8,12},{1,5},{5,9},{9,13},{2,6},{6,10},{10,14},{3,7},{... | collective-permute-start | bytes 3538952 | tf_op jit(solution)/shard_map/ppermute | solution.py:19
  324.7 2.8 fusion.21
  327.5 1.3 collective-permute-start.12
  328.8 2.8 fusion.3
  331.6 5.7 %collective-permute-start.11 = (bf16[768,768]{1,0:T(8,128)(2,1)}, bf16[768,768]{1,0:T(8,128)(2,1)}, u32[]{:S(2)}, u32[]{:S(2)}) collective-permute-start(bf16[768,768]{1,0:T(8,128)(2,1)} %fusion), channel_id=1, source_target_pairs={{0,4},{4,8},{8,12},{1,5},{5,9},{9,13},{2,6},{6,10},{10,14},{3,7},{... | collective-permute-start | bytes 3538952 | tf_op jit(solution)/shard_map/ppermute | solution.py:19
  337.3 2.8 fusion.9
  340.1 2.9 fusion.55
  343.5 2.0 copy.29
  345.5 1.8 multiply_convert_fusion
  347.3 1.1 fusion.92
  348.4 25.6 %collective-permute-done.11 = bf16[768,768]{1,0:T(8,128)(2,1)} collective-permute-done((bf16[768,768]{1,0:T(8,128)(2,1)}, bf16[768,768]{1,0:T(8,128)(2,1)}, u32[]{:S(2)}, u32[]{:S(2)}) %collective-permute-start.11) | collective-permute-done | bytes 1179680 | tf_op jit(solution)/shard_map/ppermute | solution.py:19
  374.0 1.3 constant_dynamic-update-slice_fusion.5
  375.4 1.3 constant_dynamic-update-slice_fusion.4
  376.7 2.5 constant_dynamic-update-slice_fusion.2
  379.2 2.4 constant_dynamic-update-slice_fusion.1
  381.6 1.3 constant_dynamic-update-slice_fusion.3.v_ref
  382.9 3.3 constant_dynamic-update-slice_fusion.k_ref
  386.2 17.7 %shard_map.92 = bf16[384,768]{1,0:T(8,128)(2,1)} custom-call(s32[3,8]{1,0:T(4,128)} %get-tuple-element.40.kb_ref, s32[3]{0:T(128)} %dynamic_slice.107.lim_ref, bf16[384,768]{1,0:T(8,128)(2,1)} %get-tuple-element.38.q_ref, bf16[2304,768]{1,0:T(8,128)(2,1)} %constant_dynamic-update-slice_fusion.k_ref, bf16[2304,768]{1,0:T(8,128)(2,1)} %copy-done.2), custom_call_target="tpu_custom_call" | custom-call | tf_op jit(solution)/shard_map/pallas_call | solution.py:89
  404.0 18.1 %shard_map.91 = bf16[384,768]{1,0:T(8,128)(2,1)} custom-call(s32[3,8]{1,0:T(4,128)} %get-tuple-element.39.kb_ref, s32[3]{0:T(128)} %dynamic_slice.107.lim_ref, bf16[384,768]{1,0:T(8,128)(2,1)} %get-tuple-element.37.q_ref, bf16[2304,768]{1,0:T(8,128)(2,1)} %constant_dynamic-update-slice_fusion.k_ref, bf16[2304,768]{1,0:T(8,128)(2,1)} %copy-done.2), custom_call_target="tpu_custom_call" | custom-call | tf_op jit(solution)/shard_map/pallas_call | solution.py:89
  422.1 3.5 constant_dynamic-slice_fusion.1
  425.6 1.5 collective-permute-start.15
  427.6 1.5 collective-permute-start.14
  429.1 21.3 %collective-permute-done.15 = bf16[768,640]{1,0:T(8,128)(2,1)S(1)} collective-permute-done((bf16[768,640]{1,0:T(8,128)(2,1)}, bf16[768,640]{1,0:T(8,128)(2,1)S(1)}, u32[]{:S(2)}, u32[]{:S(2)}) %collective-permute-start.15) | collective-permute-done | bytes 983072 | tf_op jit(solution)/shard_map/ppermute | solution.py:115
  450.5 1.8 fusion.60
  452.3 19.2 %collective-permute-done.13 = bf16[768,640]{1,0:T(8,128)(2,1)S(1)} collective-permute-done((bf16[768,640]{1,0:T(8,128)(2,1)}, bf16[768,640]{1,0:T(8,128)(2,1)S(1)}, u32[]{:S(2)}, u32[]{:S(2)}) %collective-permute-start.13) | collective-permute-done | bytes 983072 | tf_op jit(solution)/shard_map/ppermute | solution.py:115
  471.5 1.7 fusion.63
  473.9 16.3 %collective-permute-done.14 = bf16[768,640]{1,0:T(8,128)(2,1)} collective-permute-done((bf16[768,640]{1,0:T(8,128)(2,1)}, bf16[768,640]{1,0:T(8,128)(2,1)}, u32[]{:S(2)}, u32[]{:S(2)}) %collective-permute-start.14) | collective-permute-done | bytes 983072 | tf_op jit(solution)/shard_map/ppermute | solution.py:115
  490.2 1.9 fusion.39
  492.1 2.0 fusion.97
  494.1 1.2 fusion.2
  495.3 5.0 fusion.96
  502.2 1.9 fusion.38
  504.4 1.4 pad_maximum_fusion
  (88 shorter events, 11.9 us)
Async XLA Ops:
  6.5 2.5 copy-start
  6.5 81.8 %all-gather.9.cloned.1.call-start = ((), (), s32[]{:S(2)}) async-start(), calls=%async_computation.1 | async-start | bytes 4915200 | tf_op jit(solution)/shard_map/all_gather | solution.py:103
  9.0 155.8 %all-gather.7.cloned.1.call-start = ((), (), s32[]{:S(2)}) async-start(), calls=%async_computation | async-start | bytes 4915200 | tf_op jit(solution)/shard_map/all_gather | solution.py:103
  10.2 253.1 %all-gather.11.cloned.1.call-start = ((), (), s32[]{:S(2)}) async-start(), calls=%async_computation.2 | async-start | bytes 4915200 | tf_op jit(solution)/shard_map/all_gather | solution.py:103
  13.2 304.6 %all-gather.13.cloned.1.call-start = ((), (), s32[]{:S(2)}) async-start(), calls=%async_computation.3 | async-start | bytes 4915200 | tf_op jit(solution)/shard_map/all_gather | solution.py:103
  16.3 434.2 %all-gather.17.cloned.1.call-start = ((), (), s32[]{:S(2)}) async-start(), calls=%async_computation.5 | async-start | bytes 2949120 | tf_op jit(solution)/shard_map/all_gather | solution.py:160
  16.4 3.7 copy-start.14
  20.1 2.9 copy-start.15
  20.1 3.5 copy-start.18
  91.8 165.0 %collective-permute-start.3 = (bf16[1280,384]{1,0:T(8,128)(2,1)}, bf16[1280,384]{1,0:T(8,128)(2,1)}, u32[]{:S(2)}, u32[]{:S(2)}) collective-permute-start(bf16[1280,384]{1,0:T(8,128)(2,1)} %get-tuple-element.27), channel_id=1, source_target_pairs={{0,16},{16,0},{1,17},{17,1},{2,18},{18,2},{3,19},{19,3},{4,20},{20... | collective-permute-start | bytes 2949128 | tf_op jit(solution)/shard_map/ppermute | solution.py:115
  93.3 145.4 %collective-permute-start.5 = (bf16[1280,384]{1,0:T(8,128)(2,1)}, bf16[1280,384]{1,0:T(8,128)(2,1)}, u32[]{:S(2)}, u32[]{:S(2)}) collective-permute-start(bf16[1280,384]{1,0:T(8,128)(2,1)} %get-tuple-element.28), channel_id=1, source_target_pairs={{0,16},{16,0},{1,17},{17,1},{2,18},{18,2},{3,19},{19,3},{4,20},{20... | collective-permute-start | bytes 2949128 | tf_op jit(solution)/shard_map/ppermute | solution.py:115
  164.9 5.8 %copy-start.11 = (bf16[5120,384]{1,0:T(8,128)(2,1)S(1)}, bf16[5120,384]{1,0:T(8,128)(2,1)}, u32[]{:S(2)}) copy-start(bf16[5120,384]{1,0:T(8,128)(2,1)} %all-gather.7.cloned.1.call-done) | copy-start | bytes 11796484
  167.1 67.8 %collective-permute-start = (bf16[1280,384]{1,0:T(8,128)(2,1)S(1)}, bf16[1280,384]{1,0:T(8,128)(2,1)S(1)}, u32[]{:S(2)}, u32[]{:S(2)}) collective-permute-start(bf16[1280,384]{1,0:T(8,128)(2,1)S(1)} %get-tuple-element.30), channel_id=1, source_target_pairs={{0,16},{16,0},{1,17},{17,1},{2,18},{18,2},{3,19},{19,3},{4,20},{20... | collective-permute-start | bytes 2949128 | tf_op jit(solution)/shard_map/ppermute | solution.py:115
  168.6 44.2 %collective-permute-start.2 = (bf16[1280,384]{1,0:T(8,128)(2,1)S(1)}, bf16[1280,384]{1,0:T(8,128)(2,1)S(1)}, u32[]{:S(2)}, u32[]{:S(2)}) collective-permute-start(bf16[1280,384]{1,0:T(8,128)(2,1)S(1)} %get-tuple-element.31), channel_id=1, source_target_pairs={{0,16},{16,0},{1,17},{17,1},{2,18},{18,2},{3,19},{19,3},{4,20},{20... | collective-permute-start | bytes 2949128 | tf_op jit(solution)/shard_map/ppermute | solution.py:115
  169.2 8.4 %slice-start = ((s8[7864320]{0:T(1024)(128)(4,1)}), s8[4194304]{0:T(1024)(128)(4,1)S(1)}, s32[]{:S(2)}) async-start(s8[7864320]{0:T(1024)(128)(4,1)} %bitcast.50), calls=%async_computation.6 | async-start | bytes 8388608
  169.2 8.4 %slice-start.1 = ((s8[7864320]{0:T(1024)(128)(4,1)}), s8[3670016]{0:T(1024)(128)(4,1)S(1)}, s32[]{:S(2)}) async-start(s8[7864320]{0:T(1024)(128)(4,1)} %bitcast.50), calls=%async_computation.7 | async-start | bytes 7340032
  169.2 8.5 %copy-start.10 = (bf16[5120,384]{1,0:T(8,128)(2,1)S(1)}, bf16[5120,384]{1,0:T(8,128)(2,1)}, u32[]{:S(2)}) copy-start(bf16[5120,384]{1,0:T(8,128)(2,1)} %all-gather.9.cloned.1.call-done) | copy-start | bytes 11796484
  169.2 64.7 %collective-permute-start.1 = (bf16[1280,384]{1,0:T(8,128)(2,1)S(1)}, bf16[1280,384]{1,0:T(8,128)(2,1)S(1)}, u32[]{:S(2)}, u32[]{:S(2)}) collective-permute-start(bf16[1280,384]{1,0:T(8,128)(2,1)S(1)} %get-tuple-element.32), channel_id=1, source_target_pairs={{0,16},{16,0},{1,17},{17,1},{2,18},{18,2},{3,19},{19,3},{4,20},{20... | collective-permute-start | bytes 2949128 | tf_op jit(solution)/shard_map/ppermute | solution.py:115
  212.9 41.0 %collective-permute-start.4 = (bf16[1280,384]{1,0:T(8,128)(2,1)}, bf16[1280,384]{1,0:T(8,128)(2,1)}, u32[]{:S(2)}, u32[]{:S(2)}) collective-permute-start(bf16[1280,384]{1,0:T(8,128)(2,1)} %get-tuple-element.29), channel_id=1, source_target_pairs={{0,16},{16,0},{1,17},{17,1},{2,18},{18,2},{3,19},{19,3},{4,20},{20... | collective-permute-start | bytes 2949128 | tf_op jit(solution)/shard_map/ppermute | solution.py:115
  215.4 19.6 %copy-start.12 = (f32[768,384]{0,1:T(8,128)S(1)}, f32[768,384]{0,1:T(8,128)}, u32[]{:S(2)}) copy-start(f32[768,384]{0,1:T(8,128)} %fusion.25) | copy-start | bytes 3538948
  256.8 3.2 copy-start.13
  256.8 4.5 copy-start.16
  260.0 2.1 copy-start.3
  263.3 6.7 %copy-start.9 = (bf16[5120,384]{1,0:T(8,128)(2,1)S(1)}, bf16[5120,384]{1,0:T(8,128)(2,1)}, u32[]{:S(2)}) copy-start(bf16[5120,384]{1,0:T(8,128)(2,1)} %all-gather.11.cloned.1.call-done) | copy-start | bytes 11796484
  266.5 73.5 %collective-permute-start.6 = (bf16[1280,384]{1,0:T(8,128)(2,1)S(1)}, bf16[1280,384]{1,0:T(8,128)(2,1)}, u32[]{:S(2)}, u32[]{:S(2)}) collective-permute-start(bf16[1280,384]{1,0:T(8,128)(2,1)S(1)} %get-tuple-element.24), channel_id=1, source_target_pairs={{0,16},{16,0},{1,17},{17,1},{2,18},{18,2},{3,19},{19,3},{4,20},{20... | collective-permute-start | bytes 2949128 | tf_op jit(solution)/shard_map/ppermute | solution.py:115
  268.0 59.5 %collective-permute-start.8 = (bf16[1280,384]{1,0:T(8,128)(2,1)}, bf16[1280,384]{1,0:T(8,128)(2,1)}, u32[]{:S(2)}, u32[]{:S(2)}) collective-permute-start(bf16[1280,384]{1,0:T(8,128)(2,1)} %get-tuple-element.25), channel_id=1, source_target_pairs={{0,16},{16,0},{1,17},{17,1},{2,18},{18,2},{3,19},{19,3},{4,20},{20... | collective-permute-start | bytes 2949128 | tf_op jit(solution)/shard_map/ppermute | solution.py:115
  268.5 63.1 %collective-permute-start.7 = (bf16[1280,384]{1,0:T(8,128)(2,1)S(1)}, bf16[1280,384]{1,0:T(8,128)(2,1)}, u32[]{:S(2)}, u32[]{:S(2)}) collective-permute-start(bf16[1280,384]{1,0:T(8,128)(2,1)S(1)} %get-tuple-element.26), channel_id=1, source_target_pairs={{0,16},{16,0},{1,17},{17,1},{2,18},{18,2},{3,19},{19,3},{4,20},{20... | collective-permute-start | bytes 2949128 | tf_op jit(solution)/shard_map/ppermute | solution.py:115
  317.8 65.1 %collective-permute-start.10 = (bf16[768,768]{1,0:T(8,128)(2,1)}, bf16[768,768]{1,0:T(8,128)(2,1)}, u32[]{:S(2)}, u32[]{:S(2)}) collective-permute-start(bf16[768,768]{1,0:T(8,128)(2,1)} %multiply_convert_fusion.1), channel_id=1, source_target_pairs={{4,0},{8,4},{12,8},{5,1},{9,5},{13,9},{6,2},{10,6},{14,10},{7,3},{... | collective-permute-start | bytes 3538952 | tf_op jit(solution)/shard_map/ppermute | solution.py:19
  319.1 57.6 %collective-permute-start.9 = (bf16[768,768]{1,0:T(8,128)(2,1)}, bf16[768,768]{1,0:T(8,128)(2,1)}, u32[]{:S(2)}, u32[]{:S(2)}) collective-permute-start(bf16[768,768]{1,0:T(8,128)(2,1)} %multiply_convert_fusion.1), channel_id=1, source_target_pairs={{0,4},{4,8},{8,12},{1,5},{5,9},{9,13},{2,6},{6,10},{10,14},{3,7},{... | collective-permute-start | bytes 3538952 | tf_op jit(solution)/shard_map/ppermute | solution.py:19
  327.5 54.1 %collective-permute-start.12 = (bf16[768,768]{1,0:T(8,128)(2,1)}, bf16[768,768]{1,0:T(8,128)(2,1)}, u32[]{:S(2)}, u32[]{:S(2)}) collective-permute-start(bf16[768,768]{1,0:T(8,128)(2,1)} %fusion), channel_id=1, source_target_pairs={{4,0},{8,4},{12,8},{5,1},{9,5},{13,9},{6,2},{10,6},{14,10},{7,3},{... | collective-permute-start | bytes 3538952 | tf_op jit(solution)/shard_map/ppermute | solution.py:19
  331.6 42.4 %collective-permute-start.11 = (bf16[768,768]{1,0:T(8,128)(2,1)}, bf16[768,768]{1,0:T(8,128)(2,1)}, u32[]{:S(2)}, u32[]{:S(2)}) collective-permute-start(bf16[768,768]{1,0:T(8,128)(2,1)} %fusion), channel_id=1, source_target_pairs={{0,4},{4,8},{8,12},{1,5},{5,9},{9,13},{2,6},{6,10},{10,14},{3,7},{... | collective-permute-start | bytes 3538952 | tf_op jit(solution)/shard_map/ppermute | solution.py:19
  343.5 2.0 copy-start.17
  382.9 3.3 copy-start.2
  403.9 91.4 %all-gather.15.cloned.1.call-start = ((), (), s32[]{:S(2)}) async-start(), calls=%async_computation.4 | async-start | bytes 2949120 | tf_op jit(solution)/shard_map/all_gather | solution.py:160
  425.6 24.8 %collective-permute-start.15 = (bf16[768,640]{1,0:T(8,128)(2,1)}, bf16[768,640]{1,0:T(8,128)(2,1)S(1)}, u32[]{:S(2)}, u32[]{:S(2)}) collective-permute-start(bf16[768,640]{1,0:T(8,128)(2,1)} %get-tuple-element.22), channel_id=1, source_target_pairs={{0,16},{16,0},{1,17},{17,1},{2,18},{18,2},{3,19},{19,3},{4,20},{20... | collective-permute-start | bytes 2949128 | tf_op jit(solution)/shard_map/ppermute | solution.py:115
  427.1 44.4 %collective-permute-start.13 = (bf16[768,640]{1,0:T(8,128)(2,1)}, bf16[768,640]{1,0:T(8,128)(2,1)S(1)}, u32[]{:S(2)}, u32[]{:S(2)}) collective-permute-start(bf16[768,640]{1,0:T(8,128)(2,1)} %get-tuple-element.23), channel_id=1, source_target_pairs={{0,16},{16,0},{1,17},{17,1},{2,18},{18,2},{3,19},{19,3},{4,20},{20... | collective-permute-start | bytes 2949128 | tf_op jit(solution)/shard_map/ppermute | solution.py:115
  427.6 62.6 %collective-permute-start.14 = (bf16[768,640]{1,0:T(8,128)(2,1)}, bf16[768,640]{1,0:T(8,128)(2,1)}, u32[]{:S(2)}, u32[]{:S(2)}) collective-permute-start(bf16[768,640]{1,0:T(8,128)(2,1)} %get-tuple-element.21), channel_id=1, source_target_pairs={{0,16},{16,0},{1,17},{17,1},{2,18},{18,2},{3,19},{19,3},{4,20},{20... | collective-permute-start | bytes 2949128 | tf_op jit(solution)/shard_map/ppermute | solution.py:115
  429.1 44.1 %copy-start.4 = (bf16[768,640]{1,0:T(8,128)(2,1)S(1)}, bf16[768,640]{1,0:T(8,128)(2,1)}, u32[]{:S(2)}) copy-start(bf16[768,640]{1,0:T(8,128)(2,1)} %get-tuple-element.20) | copy-start | bytes 2949124
  450.4 22.8 %copy-start.7 = (bf16[384,3072]{1,0:T(8,128)(2,1)S(1)}, bf16[384,3072]{1,0:T(8,128)(2,1)}, u32[]{:S(2)}) copy-start(bf16[384,3072]{1,0:T(8,128)(2,1)} %all-gather.17.cloned.1.call-done) | copy-start | bytes 7077892
  473.9 18.2 %copy-start.8 = (bf16[3072,640]{1,0:T(8,128)(2,1)S(1)}, bf16[3072,640]{1,0:T(8,128)(2,1)}, u32[]{:S(2)}) copy-start(bf16[3072,640]{1,0:T(8,128)(2,1)} %all-gather.13.cloned.1.call-done) | copy-start | bytes 11796484
  495.3 5.0 copy-start.6
  502.2 2.2 copy-start.5
  504.2 2.0 copy-start.1
Sparse Core Ops, SparseCore 0:
  9.1 79.1 all-gather.8
  89.9 74.9 all-gather.6
  166.4 74.9 all-gather.10
  242.8 74.9 all-gather.12
  404.1 25.5 all-gather.16
  431.1 23.9 all-gather.14
where the time goes:
time: 514 us; the launch traced here: 513 us
  waiting for transfers between devices  321 us (62%)
  matrix products  64.6 us (13%)
  local copies, waits for them, and re-layouts  41.6 us (8%)
  Pallas kernels  35.8 us (7%)
  starting transfers between devices  28.1 us (5%)
  between operations  14.1 us (3%)
  other arithmetic  8.29 us (2%)
    all_gather x4, waiting for transfers between devices, fetch(): return (lax.all_gather(mine, 'frames', axis=0, tiled=True), other)  177 us
    ppermute x12, waiting for transfers between devices, trade(): recv.append(lax.ppermute(part, 'clips', [(0, 1), (1, 0)]))  118 us
    pallas_call x2, Pallas kernels, attend(): pl.pallas_call(functools.partial(attend_kernel, first_tile=first_tile), g...  35.8 us
    dot_general x15, matrix products, split_dot(): jnp.dot(lax.dynamic_slice_in_dim(x, at * rows, rows, 1), part, preferred_...  29.3 us
    ppermute x4, waiting for transfers between devices, shifted(): return lax.ppermute(value, axis, pairs)  25.6 us
    dot_general x5, matrix products, split_dot(): own = jnp.dot(x, got, preferred_element_type=jnp.float32)  24.6 us
    ppermute x12, starting transfers between devices, trade(): recv.append(lax.ppermute(part, 'clips', [(0, 1), (1, 0)]))  14.1 us
    ppermute x4, starting transfers between devices, shifted(): return lax.ppermute(value, axis, pairs)  13.8 us
  transfers between devices with their start and end apart: 22, of which 10 were waited for; matrix products, arithmetic and copies ran while one was open for 19% of the time, Pallas kernels for 4%

commit v1 on v0

--- a/solution.py
+++ b/solution.py
@@ -27,9 +27,18 @@
     return (normed * gain).astype(jnp.bfloat16)
 
 
-def attend_kernel(kb_ref, lim_ref, q_ref, k_ref, v_ref, o_ref, *, first_tile):
+def attend_kernel(kb_ref, lim_ref, q_ref, k0, k1, k2, v0, v1, v2, o_ref, *, first_tile):
+    def load(refs, b):
+        slab = (b >= slab_tiles).astype(jnp.int32) + (b >= 2 * slab_tiles).astype(jnp.int32)
+        at = pl.ds(pl.multiple_of((b - slab * slab_tiles) * TILE, TILE), TILE)
+        return lax.cond(
+            slab == 1,
+            lambda: refs[1][at, :],
+            lambda: lax.cond(slab == 0, lambda: refs[0][at, :], lambda: refs[2][at, :]),
+        )
+
     tiles = q_ref.shape[0] // TILE
-    slab_tiles = k_ref.shape[0] // (3 * TILE)
+    slab_tiles = k0.shape[0] // TILE
     picks = kb_ref.shape[1]
     scale = 1.0 / math.sqrt(HEAD_DIM)
     lanes = lax.broadcasted_iota(jnp.int32, (1, TILE), 1)
@@ -41,7 +50,7 @@
         scores = []
         for j in range(picks):
             b = kb_ref[i, j]
-            k = k_ref[pl.ds(pl.multiple_of(b * TILE, TILE), TILE), :]
+            k = load((k0, k1, k2), b)
             s = lax.dot_general(
                 q, k, (((1,), (1,)), ((), ())), preferred_element_type=jnp.float32
             )
@@ -61,7 +70,7 @@
         acc = None
         for j in range(picks):
             b = kb_ref[i, j]
-            v = v_ref[pl.ds(pl.multiple_of(b * TILE, TILE), TILE), :]
+            v = load((v0, v1, v2), b)
             w = (expo[j] / total).astype(jnp.bfloat16)
             part = jnp.dot(w, v, preferred_element_type=jnp.float32)
             acc = part if acc is None else acc + part
@@ -74,16 +83,14 @@
 
 def attend(query, keys, values, blocks, limits, first_tile=0, interpret=False):
     rows, cols = query.shape
-    window = keys.shape[0]
+    window = keys[0].shape[0]
     heads = cols // HEAD_DIM
     spec = pltpu.PrefetchScalarGridSpec(
         num_scalar_prefetch=2,
         grid=(heads,),
         in_specs=[
             pl.BlockSpec((rows, HEAD_DIM), lambda h, kb, lim: (0, h)),
-            pl.BlockSpec((window, HEAD_DIM), lambda h, kb, lim: (0, h)),
-            pl.BlockSpec((window, HEAD_DIM), lambda h, kb, lim: (0, h)),
-        ],
+        ] + [pl.BlockSpec((window, HEAD_DIM), lambda h, kb, lim: (0, h))] * 6,
         out_specs=pl.BlockSpec((rows, HEAD_DIM), lambda h, kb, lim: (0, h)),
     )
     return pl.pallas_call(
@@ -91,7 +98,7 @@
         grid_spec=spec,
         out_shape=jax.ShapeDtypeStruct((rows, cols), jnp.bfloat16),
         interpret=interpret,
-    )(blocks.astype(jnp.int32), limits.astype(jnp.int32), query, keys, values)
+    )(blocks.astype(jnp.int32), limits.astype(jnp.int32), query, *keys, *values)
 
 
 def fetch(piece):
@@ -145,8 +152,8 @@
     o_rows = trade(o_got)
     before = shifted((keys, values), "frames", 1)
     after = shifted((keys, values), "frames", -1)
-    key_window = jnp.concatenate([before[0], keys, after[0]], axis=0)
-    value_window = jnp.concatenate([before[1], values, after[1]], axis=0)
+    key_window = (before[0], keys, after[0])
+    value_window = (before[1], values, after[1])
     position = lax.axis_index("frames")
     zero = jnp.zeros((1,), jnp.int32)
     count_pad = jnp.concatenate([zero, slab_counts, zero], axis=0)

time: 514 us -> 546 us (1.062)
  Pallas kernels: 35.8 us -> 78.3 us
  local copies, waits for them, and re-layouts: 41.6 us -> 33 us
    pallas_call x2, Pallas kernels: 35.8 us -> 78.3 us  [attend(): pl.pallas_call(functools.partial(attend_kernel, first_tile=first_tile), g...]
    unnamed x46, local copies, waits for them, and re-layouts: 8.71 us -> 3.15 us
  transfers between devices with their start and end apart: 22 -> 22, of which waited for: 10 -> 11; matrix products, arithmetic and copies ran while one was open for 19% -> 17% of each run, Pallas kernels for 4% -> 7%
where the time goes in v1:
time: 546 us; the launch traced here: 545 us
  waiting for transfers between devices  318 us (58%)
  Pallas kernels  78.3 us (14%)
  matrix products  65.5 us (12%)
  local copies, waits for them, and re-layouts  33 us (6%)
  starting transfers between devices  28.3 us (5%)
  between operations  14.1 us (3%)
  other arithmetic  7.64 us (1%)
    all_gather x4, waiting for transfers between devices, fetch(): return (lax.all_gather(mine, 'frames', axis=0, tiled=True), other)  176 us
    ppermute x12, waiting for transfers between devices, trade(): recv.append(lax.ppermute(part, 'clips', [(0, 1), (1, 0)]))  119 us
    pallas_call x2, Pallas kernels, attend(): pl.pallas_call(functools.partial(attend_kernel, first_tile=first_tile), g...  78.3 us
    dot_general x15, matrix products, split_dot(): jnp.dot(lax.dynamic_slice_in_dim(x, at * rows, rows, 1), part, preferred_...  28.2 us
    dot_general x5, matrix products, split_dot(): own = jnp.dot(x, got, preferred_element_type=jnp.float32)  25.6 us
    ppermute x4, waiting for transfers between devices, shifted(): return lax.ppermute(value, axis, pairs)  22.5 us
    ppermute x12, starting transfers between devices, trade(): recv.append(lax.ppermute(part, 'clips', [(0, 1), (1, 0)]))  14.3 us
    ppermute x4, starting transfers between devices, shifted(): return lax.ppermute(value, axis, pairs)  13.8 us
  transfers between devices with their start and end apart: 22, of which 11 were waited for; matrix products, arithmetic and copies ran while one was open for 17% of the time, Pallas kernels for 7%

profile of v1, /device:TPU:0, one launch (start us, length us, event | category | flops | bytes accessed | tf_op | source)
XLA Modules:
  0.0 544.9 jit_solution(10887894360611772048)
XLA Ops:
  6.5 2.4 constant_dynamic-slice_fusion.13
  9.0 1.1 constant_dynamic-slice_fusion.17
  10.2 3.0 constant_dynamic-slice_fusion.8
  13.2 2.6 constant_dynamic-slice_fusion.3
  16.0 3.7 fusion.25
  19.7 3.9 fusion.23
  24.9 63.4 %all-gather.9.cloned.1.call-done = bf16[5120,384]{1,0:T(8,128)(2,1)} async-done(((bf16[1280,384]{1,0:T(8,128)(2,1)}), bf16[5120,384]{1,0:T(8,128)(2,1)}) %all-gather.9.cloned.1.call-update) | async-done | bytes 3932176 | tf_op jit(solution)/shard_map/all_gather | solution.py:110
  88.3 3.5 constant_dynamic-slice_fusion.12
  91.7 1.5 collective-permute-start.3
  93.8 71.1 %all-gather.7.cloned.1.call-done = bf16[5120,384]{1,0:T(8,128)(2,1)} async-done(((bf16[1280,384]{1,0:T(8,128)(2,1)}), bf16[5120,384]{1,0:T(8,128)(2,1)}) %all-gather.7.cloned.1.call-update) | async-done | bytes 3932176 | tf_op jit(solution)/shard_map/all_gather | solution.py:110
  164.8 2.2 constant_dynamic-slice_fusion.16
  167.1 1.5 collective-permute-start
  169.2 1.5 collective-permute-start.1
  170.6 6.9 %fusion.98 = f32[384,768]{1,0:T(8,128)S(1)} fusion(bf16[5120,384]{1,0:T(8,128)(2,1)S(1)} %copy-done.12, bf16[768,5120]{1,0:T(8,128)(2,1)} %param.9), kind=kOutput, calls=%fused_computation.114 | convolution fusion | flops 3019898880 | bytes 12976128 | tf_op jit(solution)/shard_map/dot_general | solution.py:131
  177.6 5.0 convolution_bitcast_fusion
  182.7 30.1 %collective-permute-done.2 = bf16[1280,384]{1,0:T(8,128)(2,1)S(1)} collective-permute-done((bf16[1280,384]{1,0:T(8,128)(2,1)S(1)}, bf16[1280,384]{1,0:T(8,128)(2,1)S(1)}, u32[]{:S(2)}, u32[]{:S(2)}) %collective-permute-start.2) | collective-permute-done | bytes 983072 | tf_op jit(solution)/shard_map/ppermute | solution.py:122
  212.8 1.5 collective-permute-start.4
  214.3 1.0 fusion.7
  215.3 18.6 %collective-permute-done.1 = bf16[1280,384]{1,0:T(8,128)(2,1)S(1)} collective-permute-done((bf16[1280,384]{1,0:T(8,128)(2,1)S(1)}, bf16[1280,384]{1,0:T(8,128)(2,1)S(1)}, u32[]{:S(2)}, u32[]{:S(2)}) %collective-permute-start.1) | collective-permute-done | bytes 983072 | tf_op jit(solution)/shard_map/ppermute | solution.py:122
  233.9 1.0 fusion.13
  234.9 1.2 fusion.51
  236.6 2.0 copy.23
  238.6 3.0 fusion.5
  241.6 12.2 %collective-permute-done.4 = bf16[1280,384]{1,0:T(8,128)(2,1)} collective-permute-done((bf16[1280,384]{1,0:T(8,128)(2,1)}, bf16[1280,384]{1,0:T(8,128)(2,1)}, u32[]{:S(2)}, u32[]{:S(2)}) %collective-permute-start.4) | collective-permute-done | bytes 983072 | tf_op jit(solution)/shard_map/ppermute | solution.py:122
  253.8 3.0 fusion.11
  256.8 3.1 fusion.54
  260.2 1.4 copy-done.4
  261.8 4.1 constant_dynamic-slice_fusion.7
  266.0 1.5 collective-permute-start.6
  268.0 1.5 collective-permute-start.7
  269.5 6.6 %fusion.99 = f32[384,768]{1,0:T(8,128)} fusion(bf16[5120,384]{1,0:T(8,128)(2,1)S(1)} %copy-done.10, bf16[768,5120]{1,0:T(8,128)(2,1)} %param.9), kind=kOutput, calls=%fused_computation.115 | convolution fusion | flops 3019898880 | bytes 12976128 | tf_op jit(solution)/shard_map/dot_general | solution.py:131
  276.1 41.7 %all-gather.13.cloned.1.call-done = bf16[3072,640]{1,0:T(8,128)(2,1)} async-done(((bf16[768,640]{1,0:T(8,128)(2,1)}), bf16[3072,640]{1,0:T(8,128)(2,1)}) %all-gather.13.cloned.1.call-update) | async-done | bytes 3932176 | tf_op jit(solution)/shard_map/all_gather | solution.py:110
  317.8 1.3 collective-permute-start.10
  319.1 5.6 %collective-permute-start.9 = (bf16[768,768]{1,0:T(8,128)(2,1)S(1)}, bf16[768,768]{1,0:T(8,128)(2,1)}, u32[]{:S(2)}, u32[]{:S(2)}) collective-permute-start(bf16[768,768]{1,0:T(8,128)(2,1)S(1)} %multiply_convert_fusion.1.k1), channel_id=1, source_target_pairs={{0,4},{4,8},{8,12},{1,5},{5,9},{9,13},{2,6},{6,10},{10,14},{3,7},{... | collective-permute-start | bytes 3538952 | tf_op jit(solution)/shard_map/ppermute | solution.py:19
  324.7 2.9 fusion.21
  327.6 1.3 collective-permute-start.12
  328.9 2.8 fusion.3
  331.7 5.6 %collective-permute-start.11 = (bf16[768,768]{1,0:T(8,128)(2,1)S(1)}, bf16[768,768]{1,0:T(8,128)(2,1)}, u32[]{:S(2)}, u32[]{:S(2)}) collective-permute-start(bf16[768,768]{1,0:T(8,128)(2,1)S(1)} %fusion.v1), channel_id=1, source_target_pairs={{0,4},{4,8},{8,12},{1,5},{5,9},{9,13},{2,6},{6,10},{10,14},{3,7},{... | collective-permute-start | bytes 3538952 | tf_op jit(solution)/shard_map/ppermute | solution.py:19
  337.3 2.8 fusion.9
  340.1 3.0 fusion.57
  343.4 1.7 fusion.36
  345.1 3.1 copy.29
  348.2 1.8 multiply_convert_fusion
  350.1 1.1 fusion.96
  351.2 21.4 %collective-permute-done.12.v2 = bf16[768,768]{1,0:T(8,128)(2,1)} collective-permute-done((bf16[768,768]{1,0:T(8,128)(2,1)S(1)}, bf16[768,768]{1,0:T(8,128)(2,1)}, u32[]{:S(2)}, u32[]{:S(2)}) %collective-permute-start.12) | collective-permute-done | bytes 1179680 | tf_op jit(solution)/shard_map/ppermute | solution.py:19
  372.6 1.1 collective-permute-done.11.v0
  373.7 39.0 %shard_map.91 = bf16[384,768]{1,0:T(8,128)(2,1)} custom-call(s32[3,8]{1,0:T(4,128)} %get-tuple-element.39.kb_ref, s32[3]{0:T(128)} %dynamic_slice.107.lim_ref, bf16[384,768]{1,0:T(8,128)(2,1)} %get-tuple-element.37.q_ref, bf16[768,768]{1,0:T(8,128)(2,1)} %collective-permute-done.9.k0, bf16[768,768]{1,0:T(8,128)(2,1)} %copy-done.3, ...), custom_call_target="tpu_custom_call" | custom-call | tf_op jit(solution)/shard_map/pallas_call | solution.py:96
  412.7 39.3 %shard_map.92 = bf16[384,768]{1,0:T(8,128)(2,1)} custom-call(s32[3,8]{1,0:T(4,128)} %get-tuple-element.40.kb_ref, s32[3]{0:T(128)} %dynamic_slice.107.lim_ref, bf16[384,768]{1,0:T(8,128)(2,1)} %get-tuple-element.38.q_ref, bf16[768,768]{1,0:T(8,128)(2,1)} %collective-permute-done.9.k0, bf16[768,768]{1,0:T(8,128)(2,1)} %copy-done.3, ...), custom_call_target="tpu_custom_call" | custom-call | tf_op jit(solution)/shard_map/pallas_call | solution.py:96
  452.1 3.5 constant_dynamic-slice_fusion.2
  455.6 1.7 collective-permute-start.13
  457.6 1.7 collective-permute-start.14
  459.4 21.1 %collective-permute-done.13 = bf16[768,640]{1,0:T(8,128)(2,1)S(1)} collective-permute-done((bf16[768,640]{1,0:T(8,128)(2,1)}, bf16[768,640]{1,0:T(8,128)(2,1)S(1)}, u32[]{:S(2)}, u32[]{:S(2)}) %collective-permute-start.13) | collective-permute-done | bytes 983072 | tf_op jit(solution)/shard_map/ppermute | solution.py:122
  480.4 1.8 fusion.73
  482.3 19.2 %collective-permute-done.15 = bf16[768,640]{1,0:T(8,128)(2,1)S(1)} collective-permute-done((bf16[768,640]{1,0:T(8,128)(2,1)}, bf16[768,640]{1,0:T(8,128)(2,1)S(1)}, u32[]{:S(2)}, u32[]{:S(2)}) %collective-permute-start.15) | collective-permute-done | bytes 983072 | tf_op jit(solution)/shard_map/ppermute | solution.py:122
  502.1 18.1 %collective-permute-done.14 = bf16[768,640]{1,0:T(8,128)(2,1)} collective-permute-done((bf16[768,640]{1,0:T(8,128)(2,1)}, bf16[768,640]{1,0:T(8,128)(2,1)}, u32[]{:S(2)}, u32[]{:S(2)}) %collective-permute-start.14) | collective-permute-done | bytes 983072 | tf_op jit(solution)/shard_map/ppermute | solution.py:122
  520.3 1.8 fusion.71
  522.1 0.7 fusion.39
  522.8 1.4 copy-done.9
  524.2 2.0 fusion.100
  526.2 1.2 fusion.1
  527.4 5.0 fusion.101
  533.6 1.8 fusion.64
  535.5 0.7 fusion.41
  536.7 1.4 pad_maximum_fusion
  (86 shorter events, 7.4 us)
Async XLA Ops:
  6.5 2.5 copy-start
  6.5 81.7 %all-gather.9.cloned.1.call-start = ((), (), s32[]{:S(2)}) async-start(), calls=%async_computation.1 | async-start | bytes 4915200 | tf_op jit(solution)/shard_map/all_gather | solution.py:110
  9.0 155.8 %all-gather.7.cloned.1.call-start = ((), (), s32[]{:S(2)}) async-start(), calls=%async_computation | async-start | bytes 4915200 | tf_op jit(solution)/shard_map/all_gather | solution.py:110
  10.1 251.7 %all-gather.11.cloned.1.call-start = ((), (), s32[]{:S(2)}) async-start(), calls=%async_computation.2 | async-start | bytes 4915200 | tf_op jit(solution)/shard_map/all_gather | solution.py:110
  13.2 304.6 %all-gather.13.cloned.1.call-start = ((), (), s32[]{:S(2)}) async-start(), calls=%async_computation.3 | async-start | bytes 4915200 | tf_op jit(solution)/shard_map/all_gather | solution.py:110
  15.9 464.6 %all-gather.15.cloned.1.call-start = ((), (), s32[]{:S(2)}) async-start(), calls=%async_computation.4 | async-start | bytes 2949120 | tf_op jit(solution)/shard_map/all_gather | solution.py:167
  16.0 3.7 copy-start.16
  19.7 3.9 copy-start.17
  19.7 4.5 copy-start.20
  91.7 165.0 %collective-permute-start.3 = (bf16[1280,384]{1,0:T(8,128)(2,1)}, bf16[1280,384]{1,0:T(8,128)(2,1)}, u32[]{:S(2)}, u32[]{:S(2)}) collective-permute-start(bf16[1280,384]{1,0:T(8,128)(2,1)} %get-tuple-element.27), channel_id=1, source_target_pairs={{0,16},{16,0},{1,17},{17,1},{2,18},{18,2},{3,19},{19,3},{4,20},{20... | collective-permute-start | bytes 2949128 | tf_op jit(solution)/shard_map/ppermute | solution.py:122
  93.2 145.4 %collective-permute-start.5 = (bf16[1280,384]{1,0:T(8,128)(2,1)}, bf16[1280,384]{1,0:T(8,128)(2,1)}, u32[]{:S(2)}, u32[]{:S(2)}) collective-permute-start(bf16[1280,384]{1,0:T(8,128)(2,1)} %get-tuple-element.28), channel_id=1, source_target_pairs={{0,16},{16,0},{1,17},{17,1},{2,18},{18,2},{3,19},{19,3},{4,20},{20... | collective-permute-start | bytes 2949128 | tf_op jit(solution)/shard_map/ppermute | solution.py:122
  164.8 5.8 %copy-start.12 = (bf16[5120,384]{1,0:T(8,128)(2,1)S(1)}, bf16[5120,384]{1,0:T(8,128)(2,1)}, u32[]{:S(2)}) copy-start(bf16[5120,384]{1,0:T(8,128)(2,1)} %all-gather.7.cloned.1.call-done) | copy-start | bytes 11796484
  167.1 67.8 %collective-permute-start = (bf16[1280,384]{1,0:T(8,128)(2,1)S(1)}, bf16[1280,384]{1,0:T(8,128)(2,1)S(1)}, u32[]{:S(2)}, u32[]{:S(2)}) collective-permute-start(bf16[1280,384]{1,0:T(8,128)(2,1)S(1)} %get-tuple-element.30), channel_id=1, source_target_pairs={{0,16},{16,0},{1,17},{17,1},{2,18},{18,2},{3,19},{19,3},{4,20},{20... | collective-permute-start | bytes 2949128 | tf_op jit(solution)/shard_map/ppermute | solution.py:122
  168.6 44.2 %collective-permute-start.2 = (bf16[1280,384]{1,0:T(8,128)(2,1)S(1)}, bf16[1280,384]{1,0:T(8,128)(2,1)S(1)}, u32[]{:S(2)}, u32[]{:S(2)}) collective-permute-start(bf16[1280,384]{1,0:T(8,128)(2,1)S(1)} %get-tuple-element.31), channel_id=1, source_target_pairs={{0,16},{16,0},{1,17},{17,1},{2,18},{18,2},{3,19},{19,3},{4,20},{20... | collective-permute-start | bytes 2949128 | tf_op jit(solution)/shard_map/ppermute | solution.py:122
  169.2 8.4 %slice-start = ((s8[7864320]{0:T(1024)(128)(4,1)}), s8[4194304]{0:T(1024)(128)(4,1)S(1)}, s32[]{:S(2)}) async-start(s8[7864320]{0:T(1024)(128)(4,1)} %bitcast.50), calls=%async_computation.6 | async-start | bytes 8388608
  169.2 8.4 %slice-start.1 = ((s8[7864320]{0:T(1024)(128)(4,1)}), s8[3670016]{0:T(1024)(128)(4,1)S(1)}, s32[]{:S(2)}) async-start(s8[7864320]{0:T(1024)(128)(4,1)} %bitcast.50), calls=%async_computation.7 | async-start | bytes 7340032
  169.2 8.5 %copy-start.11 = (bf16[5120,384]{1,0:T(8,128)(2,1)S(1)}, bf16[5120,384]{1,0:T(8,128)(2,1)}, u32[]{:S(2)}) copy-start(bf16[5120,384]{1,0:T(8,128)(2,1)} %all-gather.9.cloned.1.call-done) | copy-start | bytes 11796484
  169.2 64.7 %collective-permute-start.1 = (bf16[1280,384]{1,0:T(8,128)(2,1)S(1)}, bf16[1280,384]{1,0:T(8,128)(2,1)S(1)}, u32[]{:S(2)}, u32[]{:S(2)}) collective-permute-start(bf16[1280,384]{1,0:T(8,128)(2,1)S(1)} %get-tuple-element.32), channel_id=1, source_target_pairs={{0,16},{16,0},{1,17},{17,1},{2,18},{18,2},{3,19},{19,3},{4,20},{20... | collective-permute-start | bytes 2949128 | tf_op jit(solution)/shard_map/ppermute | solution.py:122
  212.8 41.0 %collective-permute-start.4 = (bf16[1280,384]{1,0:T(8,128)(2,1)}, bf16[1280,384]{1,0:T(8,128)(2,1)}, u32[]{:S(2)}, u32[]{:S(2)}) collective-permute-start(bf16[1280,384]{1,0:T(8,128)(2,1)} %get-tuple-element.29), channel_id=1, source_target_pairs={{0,16},{16,0},{1,17},{17,1},{2,18},{18,2},{3,19},{19,3},{4,20},{20... | collective-permute-start | bytes 2949128 | tf_op jit(solution)/shard_map/ppermute | solution.py:122
  215.3 19.6 %copy-start.14 = (f32[768,384]{0,1:T(8,128)S(1)}, f32[768,384]{0,1:T(8,128)}, u32[]{:S(2)}) copy-start(f32[768,384]{0,1:T(8,128)} %fusion.25) | copy-start | bytes 3538948
  241.6 15.2 %copy-start.13 = (f32[768,384]{1,0:T(8,128)S(1)}, f32[768,384]{1,0:T(8,128)}, u32[]{:S(2)}) copy-start(f32[768,384]{1,0:T(8,128)} %fusion.23) | copy-start | bytes 3538948
  256.8 3.1 copy-start.15
  256.8 3.4 copy-start.18
  259.9 1.7 copy-start.4
  261.6 70.1 %copy-start.2 = (bf16[768,768]{1,0:T(8,128)(2,1)}, bf16[768,768]{1,0:T(8,128)(2,1)S(1)}, u32[]{:S(2)}) copy-start(bf16[768,768]{1,0:T(8,128)(2,1)S(1)} %fusion.v1) | copy-start | bytes 3538948
  261.8 57.3 %copy-start.3 = (bf16[768,768]{1,0:T(8,128)(2,1)}, bf16[768,768]{1,0:T(8,128)(2,1)S(1)}, u32[]{:S(2)}) copy-start(bf16[768,768]{1,0:T(8,128)(2,1)S(1)} %multiply_convert_fusion.1.k1) | copy-start | bytes 3538948
  261.8 7.6 %copy-start.10 = (bf16[5120,384]{1,0:T(8,128)(2,1)S(1)}, bf16[5120,384]{1,0:T(8,128)(2,1)}, u32[]{:S(2)}) copy-start(bf16[5120,384]{1,0:T(8,128)(2,1)} %all-gather.11.cloned.1.call-done) | copy-start | bytes 11796484
  266.0 74.1 %collective-permute-start.6 = (bf16[1280,384]{1,0:T(8,128)(2,1)}, bf16[1280,384]{1,0:T(8,128)(2,1)}, u32[]{:S(2)}, u32[]{:S(2)}) collective-permute-start(bf16[1280,384]{1,0:T(8,128)(2,1)} %get-tuple-element.24), channel_id=1, source_target_pairs={{0,16},{16,0},{1,17},{17,1},{2,18},{18,2},{3,19},{19,3},{4,20},{20... | collective-permute-start | bytes 2949128 | tf_op jit(solution)/shard_map/ppermute | solution.py:122
  267.4 60.1 %collective-permute-start.8 = (bf16[1280,384]{1,0:T(8,128)(2,1)}, bf16[1280,384]{1,0:T(8,128)(2,1)}, u32[]{:S(2)}, u32[]{:S(2)}) collective-permute-start(bf16[1280,384]{1,0:T(8,128)(2,1)} %get-tuple-element.25), channel_id=1, source_target_pairs={{0,16},{16,0},{1,17},{17,1},{2,18},{18,2},{3,19},{19,3},{4,20},{20... | collective-permute-start | bytes 2949128 | tf_op jit(solution)/shard_map/ppermute | solution.py:122
  268.0 63.7 %collective-permute-start.7 = (bf16[1280,384]{1,0:T(8,128)(2,1)}, bf16[1280,384]{1,0:T(8,128)(2,1)}, u32[]{:S(2)}, u32[]{:S(2)}) collective-permute-start(bf16[1280,384]{1,0:T(8,128)(2,1)} %get-tuple-element.26), channel_id=1, source_target_pairs={{0,16},{16,0},{1,17},{17,1},{2,18},{18,2},{3,19},{19,3},{4,20},{20... | collective-permute-start | bytes 2949128 | tf_op jit(solution)/shard_map/ppermute | solution.py:122
  317.8 33.4 %collective-permute-start.10 = (bf16[768,768]{1,0:T(8,128)(2,1)S(1)}, bf16[768,768]{1,0:T(8,128)(2,1)}, u32[]{:S(2)}, u32[]{:S(2)}) collective-permute-start(bf16[768,768]{1,0:T(8,128)(2,1)S(1)} %multiply_convert_fusion.1.k1), channel_id=1, source_target_pairs={{4,0},{8,4},{12,8},{5,1},{9,5},{13,9},{6,2},{10,6},{14,10},{7,3},{... | collective-permute-start | bytes 3538952 | tf_op jit(solution)/shard_map/ppermute | solution.py:19
  319.1 32.1 %collective-permute-start.9 = (bf16[768,768]{1,0:T(8,128)(2,1)S(1)}, bf16[768,768]{1,0:T(8,128)(2,1)}, u32[]{:S(2)}, u32[]{:S(2)}) collective-permute-start(bf16[768,768]{1,0:T(8,128)(2,1)S(1)} %multiply_convert_fusion.1.k1), channel_id=1, source_target_pairs={{0,4},{4,8},{8,12},{1,5},{5,9},{9,13},{2,6},{6,10},{10,14},{3,7},{... | collective-permute-start | bytes 3538952 | tf_op jit(solution)/shard_map/ppermute | solution.py:19
  327.6 45.0 %collective-permute-start.12 = (bf16[768,768]{1,0:T(8,128)(2,1)S(1)}, bf16[768,768]{1,0:T(8,128)(2,1)}, u32[]{:S(2)}, u32[]{:S(2)}) collective-permute-start(bf16[768,768]{1,0:T(8,128)(2,1)S(1)} %fusion.v1), channel_id=1, source_target_pairs={{4,0},{8,4},{12,8},{5,1},{9,5},{13,9},{6,2},{10,6},{14,10},{7,3},{... | collective-permute-start | bytes 3538952 | tf_op jit(solution)/shard_map/ppermute | solution.py:19
  331.7 42.0 %collective-permute-start.11 = (bf16[768,768]{1,0:T(8,128)(2,1)S(1)}, bf16[768,768]{1,0:T(8,128)(2,1)}, u32[]{:S(2)}, u32[]{:S(2)}) collective-permute-start(bf16[768,768]{1,0:T(8,128)(2,1)S(1)} %fusion.v1), channel_id=1, source_target_pairs={{0,4},{4,8},{8,12},{1,5},{5,9},{9,13},{2,6},{6,10},{10,14},{3,7},{... | collective-permute-start | bytes 3538952 | tf_op jit(solution)/shard_map/ppermute | solution.py:19
  340.1 3.0 copy-start.5
  345.1 3.2 copy-start.19
  412.7 114.7 %all-gather.17.cloned.1.call-start = ((), (), s32[]{:S(2)}) async-start(), calls=%async_computation.5 | async-start | bytes 2949120 | tf_op jit(solution)/shard_map/all_gather | solution.py:167
  455.6 24.8 %collective-permute-start.13 = (bf16[768,640]{1,0:T(8,128)(2,1)}, bf16[768,640]{1,0:T(8,128)(2,1)S(1)}, u32[]{:S(2)}, u32[]{:S(2)}) collective-permute-start(bf16[768,640]{1,0:T(8,128)(2,1)} %get-tuple-element.21), channel_id=1, source_target_pairs={{0,16},{16,0},{1,17},{17,1},{2,18},{18,2},{3,19},{19,3},{4,20},{20... | collective-permute-start | bytes 2949128 | tf_op jit(solution)/shard_map/ppermute | solution.py:122
  457.3 44.2 %collective-permute-start.15 = (bf16[768,640]{1,0:T(8,128)(2,1)}, bf16[768,640]{1,0:T(8,128)(2,1)S(1)}, u32[]{:S(2)}, u32[]{:S(2)}) collective-permute-start(bf16[768,640]{1,0:T(8,128)(2,1)} %get-tuple-element.22), channel_id=1, source_target_pairs={{0,16},{16,0},{1,17},{17,1},{2,18},{18,2},{3,19},{19,3},{4,20},{20... | collective-permute-start | bytes 2949128 | tf_op jit(solution)/shard_map/ppermute | solution.py:122
  457.6 62.6 %collective-permute-start.14 = (bf16[768,640]{1,0:T(8,128)(2,1)}, bf16[768,640]{1,0:T(8,128)(2,1)}, u32[]{:S(2)}, u32[]{:S(2)}) collective-permute-start(bf16[768,640]{1,0:T(8,128)(2,1)} %get-tuple-element.23), channel_id=1, source_target_pairs={{0,16},{16,0},{1,17},{17,1},{2,18},{18,2},{3,19},{19,3},{4,20},{20... | collective-permute-start | bytes 2949128 | tf_op jit(solution)/shard_map/ppermute | solution.py:122
  480.4 21.1 %copy-start.7 = (bf16[384,3072]{1,0:T(8,128)(2,1)S(1)}, bf16[384,3072]{1,0:T(8,128)(2,1)}, u32[]{:S(2)}) copy-start(bf16[384,3072]{1,0:T(8,128)(2,1)} %all-gather.15.cloned.1.call-done) | copy-start | bytes 7077892
  522.1 2.1 copy-start.9
  527.4 5.0 copy-start.8
  535.5 1.2 copy-start.6
  536.2 1.9 copy-start.1
Sparse Core Ops, SparseCore 0:
  9.1 79.1 all-gather.8
  89.8 74.9 all-gather.6
  166.4 74.9 all-gather.10
  242.8 74.9 all-gather.12
  412.8 25.8 all-gather.14
  452.2 25.7 all-gather.16

commit v2 on v0

--- a/solution.py
+++ b/solution.py
@@ -45,6 +45,7 @@
             s = lax.dot_general(
                 q, k, (((1,), (1,)), ((), ())), preferred_element_type=jnp.float32
             )
+            s = s * scale
             slab = (b >= slab_tiles).astype(jnp.int32) + (b >= 2 * slab_tiles).astype(jnp.int32)
             limit = lim_ref[slab]
             pos = (b - slab * slab_tiles) * TILE + lanes
@@ -53,7 +54,7 @@
         for s in scores[1:]:
             top = jnp.maximum(top, s)
         top = jnp.max(top, axis=1, keepdims=True)
-        expo = [jnp.exp((s - top) * scale) for s in scores]
+        expo = [jnp.exp(s - top) for s in scores]
         total = expo[0]
         for e in expo[1:]:
             total = total + e
@@ -141,18 +142,20 @@
     values = split_dot(tokens, trade(v_got)).astype(jnp.bfloat16)
     keys, values, q_got = lax.optimization_barrier((keys, values, q_got))
     query = head_norm(split_dot(tokens, trade(q_got)), q_gain)
-    keys, values, o_got = lax.optimization_barrier((keys, values, o_got))
+    width = keys.shape[1]
+    both, o_got = lax.optimization_barrier((jnp.concatenate([keys, values], axis=1), o_got))
+    keys, values = both[:, :width], both[:, width:]
     o_rows = trade(o_got)
-    before = shifted((keys, values), "frames", 1)
-    after = shifted((keys, values), "frames", -1)
-    key_window = jnp.concatenate([before[0], keys, after[0]], axis=0)
-    value_window = jnp.concatenate([before[1], values, after[1]], axis=0)
+    before = shifted(both, "frames", 1)
+    after = shifted(both, "frames", -1)
+    key_window = jnp.concatenate([before[:, :width], keys, after[:, :width]], axis=0)
+    value_window = jnp.concatenate([before[:, width:], values, after[:, width:]], axis=0)
     position = lax.axis_index("frames")
     zero = jnp.zeros((1,), jnp.int32)
     count_pad = jnp.concatenate([zero, slab_counts, zero], axis=0)
     limits = lax.dynamic_slice_in_dim(count_pad, position, 3, 0)
     tiles = query.shape[0] // TILE
-    half = tiles // 2
+    half = tiles // 3
     mixed = []
     for lo, hi in ((0, half), (half, tiles)):
         part = attend(query[lo * TILE:hi * TILE], key_window, value_window,

time: 514 us -> 511 us (level)
  starting transfers between devices: 28.1 us -> 22 us
    slice x0 -> x3, local copies, waits for them, and re-layouts: none -> 6.5 us  [the longest x1 2.94 us: layer(): keys, values = (both[:, :width], both[:, width:])]
    unnamed x46 -> x50, local copies, waits for them, and re-layouts: 8.71 us -> 2.24 us
    ppermute x4 -> x2, starting transfers between devices: 13.8 us -> 7.61 us  [shifted(): return lax.ppermute(value, axis, pairs)]
    ppermute x4 -> x2, waiting for transfers between devices: 25.6 us -> 30.3 us  [shifted(): return lax.ppermute(value, axis, pairs)]
  transfers between devices with their start and end apart: 22 -> 20, of which waited for: 10 -> 11; matrix products, arithmetic and copies ran while one was open for 19% -> 18% of each run, Pallas kernels for 4% -> 4%
where the time goes in v2:
time: 511 us; the launch traced here: 510 us
  waiting for transfers between devices  325 us (64%)
  matrix products  62.4 us (12%)
  local copies, waits for them, and re-layouts  38.5 us (8%)
  Pallas kernels  35.1 us (7%)
  starting transfers between devices  22 us (4%)
  between operations  14.1 us (3%)
  other arithmetic  12.8 us (3%)
    all_gather x4, waiting for transfers between devices, fetch(): return (lax.all_gather(mine, 'frames', axis=0, tiled=True), other)  176 us
    ppermute x12, waiting for transfers between devices, trade(): recv.append(lax.ppermute(part, 'clips', [(0, 1), (1, 0)]))  118 us
    pallas_call x2, Pallas kernels, attend(): pl.pallas_call(functools.partial(attend_kernel, first_tile=first_tile), g...  35.1 us
    ppermute x2, waiting for transfers between devices, shifted(): return lax.ppermute(value, axis, pairs)  30.3 us
    dot_general x15, matrix products, split_dot(): jnp.dot(lax.dynamic_slice_in_dim(x, at * rows, rows, 1), part, preferred_...  26.2 us
    dot_general x5, matrix products, split_dot(): own = jnp.dot(x, got, preferred_element_type=jnp.float32)  24.8 us
    ppermute x12, starting transfers between devices, trade(): recv.append(lax.ppermute(part, 'clips', [(0, 1), (1, 0)]))  14.1 us
    dynamic_slice x4, local copies, waits for them, and re-layouts, trade(): part = lax.dynamic_slice_in_dim(got, at * rows, rows, 0)  12.9 us
  transfers between devices with their start and end apart: 20, of which 11 were waited for; matrix products, arithmetic and copies ran while one was open for 18% of the time, Pallas kernels for 4%

profile of v2, /device:TPU:0, one launch (start us, length us, event | category | flops | bytes accessed | tf_op | source)
XLA Modules:
  0.0 509.7 jit_solution(13888061790304764137)
XLA Ops:
  6.5 2.4 constant_dynamic-slice_fusion.13
  9.1 1.1 constant_dynamic-slice_fusion.17
  10.2 3.0 constant_dynamic-slice_fusion.8
  13.2 3.0 constant_dynamic-slice_fusion.3
  16.3 3.7 fusion.24
  20.0 2.9 fusion.22
  24.2 64.1 %all-gather.9.cloned.1.call-done = bf16[5120,384]{1,0:T(8,128)(2,1)} async-done(((bf16[1280,384]{1,0:T(8,128)(2,1)}), bf16[5120,384]{1,0:T(8,128)(2,1)}) %all-gather.9.cloned.1.call-update) | async-done | bytes 3932176 | tf_op jit(solution)/shard_map/all_gather | solution.py:104
  88.3 3.5 constant_dynamic-slice_fusion.12
  91.8 1.5 collective-permute-start.3
  93.8 71.0 %all-gather.7.cloned.1.call-done = bf16[5120,384]{1,0:T(8,128)(2,1)} async-done(((bf16[1280,384]{1,0:T(8,128)(2,1)}), bf16[5120,384]{1,0:T(8,128)(2,1)}) %all-gather.7.cloned.1.call-update) | async-done | bytes 3932176 | tf_op jit(solution)/shard_map/all_gather | solution.py:104
  164.8 2.2 constant_dynamic-slice_fusion.16
  167.1 1.5 collective-permute-start
  169.2 1.5 collective-permute-start.1
  170.7 6.9 %fusion.95 = f32[384,768]{1,0:T(8,128)S(1)} fusion(bf16[5120,384]{1,0:T(8,128)(2,1)S(1)} %copy-done.10, bf16[768,5120]{1,0:T(8,128)(2,1)} %param.9), kind=kOutput, calls=%fused_computation.116 | convolution fusion | flops 3019898880 | bytes 12976128 | tf_op jit(solution)/shard_map/dot_general | solution.py:125
  177.6 5.0 convolution_bitcast_fusion
  182.7 30.2 %collective-permute-done.2 = bf16[1280,384]{1,0:T(8,128)(2,1)S(1)} collective-permute-done((bf16[1280,384]{1,0:T(8,128)(2,1)S(1)}, bf16[1280,384]{1,0:T(8,128)(2,1)S(1)}, u32[]{:S(2)}, u32[]{:S(2)}) %collective-permute-start.2) | collective-permute-done | bytes 983072 | tf_op jit(solution)/shard_map/ppermute | solution.py:116
  212.8 1.5 collective-permute-start.4
  214.3 1.0 fusion.6
  215.3 18.5 %collective-permute-done.1 = bf16[1280,384]{1,0:T(8,128)(2,1)S(1)} collective-permute-done((bf16[1280,384]{1,0:T(8,128)(2,1)S(1)}, bf16[1280,384]{1,0:T(8,128)(2,1)S(1)}, u32[]{:S(2)}, u32[]{:S(2)}) %collective-permute-start.1) | collective-permute-done | bytes 983072 | tf_op jit(solution)/shard_map/ppermute | solution.py:116
  233.9 1.0 fusion.12
  234.9 1.2 fusion.47
  236.6 2.0 copy.23
  238.6 3.0 fusion.4
  241.6 12.2 %collective-permute-done.4 = bf16[1280,384]{1,0:T(8,128)(2,1)} collective-permute-done((bf16[1280,384]{1,0:T(8,128)(2,1)}, bf16[1280,384]{1,0:T(8,128)(2,1)}, u32[]{:S(2)}, u32[]{:S(2)}) %collective-permute-start.4) | collective-permute-done | bytes 983072 | tf_op jit(solution)/shard_map/ppermute | solution.py:116
  253.8 3.0 fusion.10
  256.8 3.1 fusion.50
  260.3 1.4 copy-done.2
  261.9 3.7 constant_dynamic-slice_fusion.7
  265.5 1.5 collective-permute-start.8
  267.0 5.7 %fusion.96 = f32[384,768]{1,0:T(8,128)S(1)} fusion(bf16[5120,384]{1,0:T(8,128)(2,1)S(1)} %copy-done.8, bf16[768,5120]{1,0:T(8,128)(2,1)} %param.9), kind=kOutput, calls=%fused_computation.117 | convolution fusion | flops 3019898880 | bytes 12976128 | tf_op jit(solution)/shard_map/dot_general | solution.py:125
  273.3 1.5 collective-permute-start.7
  274.8 1.6 pad_maximum_fusion.2
  276.4 41.4 %all-gather.13.cloned.1.call-done = bf16[3072,640]{1,0:T(8,128)(2,1)} async-done(((bf16[768,640]{1,0:T(8,128)(2,1)}), bf16[3072,640]{1,0:T(8,128)(2,1)}) %all-gather.13.cloned.1.call-update) | async-done | bytes 3932176 | tf_op jit(solution)/shard_map/all_gather | solution.py:104
  317.8 1.4 collective-permute-start.10
  319.2 2.9 fusion.93
  322.2 6.2 %collective-permute-start.9 = (bf16[768,1536]{1,0:T(8,128)(2,1)}, bf16[768,1536]{1,0:T(8,128)(2,1)}, u32[]{:S(2)}, u32[]{:S(2)}) collective-permute-start(bf16[768,1536]{1,0:T(8,128)(2,1)} %pad_maximum_fusion.2), channel_id=1, source_target_pairs={{0,4},{4,8},{8,12},{1,5},{5,9},{9,13},{2,6},{6,10},{10,14},{3,7},{... | collective-permute-start | bytes 7077896 | tf_op jit(solution)/shard_map/ppermute | solution.py:19
  328.4 2.5 fusion.20
  330.9 2.8 fusion.2
  333.8 2.2 fusion.8
  336.0 2.4 fusion.53
  338.7 1.9 fusion.36
  340.6 2.0 copy.29
  342.7 1.8 multiply_convert_fusion
  345.3 27.7 %collective-permute-done.10 = bf16[768,1536]{1,0:T(8,128)(2,1)} collective-permute-done((bf16[768,1536]{1,0:T(8,128)(2,1)}, bf16[768,1536]{1,0:T(8,128)(2,1)}, u32[]{:S(2)}, u32[]{:S(2)}) %collective-permute-start.10) | collective-permute-done | bytes 2359328 | tf_op jit(solution)/shard_map/ppermute | solution.py:19
  373.0 1.8 fusion.94
  374.7 2.6 collective-permute-done.9
  377.3 1.8 fusion.92
  379.1 3.3 pad_maximum_fusion
  382.4 12.5 %shard_map.91 = bf16[256,768]{1,0:T(8,128)(2,1)} custom-call(s32[2,8]{1,0:T(2,128)} %slice.30.kb_ref, s32[3]{0:T(128)} %dynamic_slice.107.lim_ref, bf16[256,768]{1,0:T(8,128)(2,1)} %slice.40.q_ref, bf16[2304,768]{1,0:T(8,128)(2,1)} %get-tuple-element.41.k_ref, bf16[2304,768]{1,0:T(8,128)(2,1)} %get-tuple-element.42.v_ref), custom_call_target="tpu_custom_call" | custom-call | tf_op jit(solution)/shard_map/pallas_call | solution.py:90
  395.6 0.9 slice.45.q_ref
  396.5 22.6 %shard_map.92 = bf16[512,768]{1,0:T(8,128)(2,1)} custom-call(s32[4,8]{1,0:T(4,128)} %slice.38.kb_ref, s32[3]{0:T(128)} %dynamic_slice.107.lim_ref, bf16[512,768]{1,0:T(8,128)(2,1)} %slice.45.q_ref, bf16[2304,768]{1,0:T(8,128)(2,1)} %get-tuple-element.41.k_ref, bf16[2304,768]{1,0:T(8,128)(2,1)} %get-tuple-element.42.v_ref), custom_call_target="tpu_custom_call" | custom-call | tf_op jit(solution)/shard_map/pallas_call | solution.py:90
  419.2 3.5 constant_dynamic-slice_fusion.1
  422.6 1.5 collective-permute-start.13
  424.7 1.5 collective-permute-start.12
  426.1 21.4 %collective-permute-done.13 = bf16[768,640]{1,0:T(8,128)(2,1)} collective-permute-done((bf16[768,640]{1,0:T(8,128)(2,1)}, bf16[768,640]{1,0:T(8,128)(2,1)}, u32[]{:S(2)}, u32[]{:S(2)}) %collective-permute-start.13) | collective-permute-done | bytes 983072 | tf_op jit(solution)/shard_map/ppermute | solution.py:116
  447.6 1.9 fusion.66
  449.5 1.5 fusion.70
  451.0 17.5 %collective-permute-done.11 = bf16[768,640]{1,0:T(8,128)(2,1)S(1)} collective-permute-done((bf16[768,640]{1,0:T(8,128)(2,1)}, bf16[768,640]{1,0:T(8,128)(2,1)S(1)}, u32[]{:S(2)}, u32[]{:S(2)}) %collective-permute-start.11) | collective-permute-done | bytes 983072 | tf_op jit(solution)/shard_map/ppermute | solution.py:116
  469.0 18.2 %collective-permute-done.12 = bf16[768,640]{1,0:T(8,128)(2,1)S(1)} collective-permute-done((bf16[768,640]{1,0:T(8,128)(2,1)}, bf16[768,640]{1,0:T(8,128)(2,1)S(1)}, u32[]{:S(2)}, u32[]{:S(2)}) %collective-permute-start.12) | collective-permute-done | bytes 983072 | tf_op jit(solution)/shard_map/ppermute | solution.py:116
  487.7 1.4 fusion.97
  489.1 1.0 fusion.56
  490.1 5.8 %fusion.98 = bf16[512,640]{1,0:T(8,128)(2,1)S(1)} fusion(bf16[512,3072]{1,0:T(8,128)(2,1)} %all-gather.17.cloned.1.call-done, bf16[3072,640]{1,0:T(8,128)(2,1)} %all-gather.13.cloned.1.call-done), kind=kOutput, calls=%fused_computation.119 | convolution fusion | flops 2013265920 | bytes 7733248 | tf_op jit(solution)/shard_map/dot_general | solution.py:125
  496.7 2.0 fusion.60
  501.5 1.4 pad_maximum_fusion.3
  (94 shorter events, 11.1 us)
Async XLA Ops:
  6.5 2.5 copy-start
  6.5 81.8 %all-gather.9.cloned.1.call-start = ((), (), s32[]{:S(2)}) async-start(), calls=%async_computation.1 | async-start | bytes 4915200 | tf_op jit(solution)/shard_map/all_gather | solution.py:104
  9.0 155.8 %all-gather.7.cloned.1.call-start = ((), (), s32[]{:S(2)}) async-start(), calls=%async_computation | async-start | bytes 4915200 | tf_op jit(solution)/shard_map/all_gather | solution.py:104
  10.1 251.7 %all-gather.11.cloned.1.call-start = ((), (), s32[]{:S(2)}) async-start(), calls=%async_computation.2 | async-start | bytes 4915200 | tf_op jit(solution)/shard_map/all_gather | solution.py:104
  13.2 304.6 %all-gather.13.cloned.1.call-start = ((), (), s32[]{:S(2)}) async-start(), calls=%async_computation.3 | async-start | bytes 4915200 | tf_op jit(solution)/shard_map/all_gather | solution.py:104
  16.2 431.4 %all-gather.15.cloned.1.call-start = ((), (), s32[]{:S(2)}) async-start(), calls=%async_computation.4 | async-start | bytes 1966080 | tf_op jit(solution)/shard_map/all_gather | solution.py:163
  16.3 3.7 copy-start.16
  20.0 2.9 copy-start.19
  20.0 3.5 copy-start.20
  91.8 165.0 %collective-permute-start.3 = (bf16[1280,384]{1,0:T(8,128)(2,1)}, bf16[1280,384]{1,0:T(8,128)(2,1)}, u32[]{:S(2)}, u32[]{:S(2)}) collective-permute-start(bf16[1280,384]{1,0:T(8,128)(2,1)} %get-tuple-element.25), channel_id=1, source_target_pairs={{0,16},{16,0},{1,17},{17,1},{2,18},{18,2},{3,19},{19,3},{4,20},{20... | collective-permute-start | bytes 2949128 | tf_op jit(solution)/shard_map/ppermute | solution.py:116
  93.3 145.4 %collective-permute-start.5 = (bf16[1280,384]{1,0:T(8,128)(2,1)}, bf16[1280,384]{1,0:T(8,128)(2,1)}, u32[]{:S(2)}, u32[]{:S(2)}) collective-permute-start(bf16[1280,384]{1,0:T(8,128)(2,1)} %get-tuple-element.26), channel_id=1, source_target_pairs={{0,16},{16,0},{1,17},{17,1},{2,18},{18,2},{3,19},{19,3},{4,20},{20... | collective-permute-start | bytes 2949128 | tf_op jit(solution)/shard_map/ppermute | solution.py:116
  164.8 5.8 %copy-start.10 = (bf16[5120,384]{1,0:T(8,128)(2,1)S(1)}, bf16[5120,384]{1,0:T(8,128)(2,1)}, u32[]{:S(2)}) copy-start(bf16[5120,384]{1,0:T(8,128)(2,1)} %all-gather.7.cloned.1.call-done) | copy-start | bytes 11796484
  167.1 67.8 %collective-permute-start = (bf16[1280,384]{1,0:T(8,128)(2,1)S(1)}, bf16[1280,384]{1,0:T(8,128)(2,1)S(1)}, u32[]{:S(2)}, u32[]{:S(2)}) collective-permute-start(bf16[1280,384]{1,0:T(8,128)(2,1)S(1)} %get-tuple-element.28), channel_id=1, source_target_pairs={{0,16},{16,0},{1,17},{17,1},{2,18},{18,2},{3,19},{19,3},{4,20},{20... | collective-permute-start | bytes 2949128 | tf_op jit(solution)/shard_map/ppermute | solution.py:116
  168.6 44.2 %collective-permute-start.2 = (bf16[1280,384]{1,0:T(8,128)(2,1)S(1)}, bf16[1280,384]{1,0:T(8,128)(2,1)S(1)}, u32[]{:S(2)}, u32[]{:S(2)}) collective-permute-start(bf16[1280,384]{1,0:T(8,128)(2,1)S(1)} %get-tuple-element.29), channel_id=1, source_target_pairs={{0,16},{16,0},{1,17},{17,1},{2,18},{18,2},{3,19},{19,3},{4,20},{20... | collective-permute-start | bytes 2949128 | tf_op jit(solution)/shard_map/ppermute | solution.py:116
  169.2 8.4 %slice-start = ((s8[7864320]{0:T(1024)(128)(4,1)}), s8[4194304]{0:T(1024)(128)(4,1)S(1)}, s32[]{:S(2)}) async-start(s8[7864320]{0:T(1024)(128)(4,1)} %bitcast.50), calls=%async_computation.6 | async-start | bytes 8388608
  169.2 8.5 %slice-start.1 = ((s8[7864320]{0:T(1024)(128)(4,1)}), s8[3670016]{0:T(1024)(128)(4,1)S(1)}, s32[]{:S(2)}) async-start(s8[7864320]{0:T(1024)(128)(4,1)} %bitcast.50), calls=%async_computation.7 | async-start | bytes 7340032
  169.2 8.5 %copy-start.9 = (bf16[5120,384]{1,0:T(8,128)(2,1)S(1)}, bf16[5120,384]{1,0:T(8,128)(2,1)}, u32[]{:S(2)}) copy-start(bf16[5120,384]{1,0:T(8,128)(2,1)} %all-gather.9.cloned.1.call-done) | copy-start | bytes 11796484
  169.2 64.7 %collective-permute-start.1 = (bf16[1280,384]{1,0:T(8,128)(2,1)S(1)}, bf16[1280,384]{1,0:T(8,128)(2,1)S(1)}, u32[]{:S(2)}, u32[]{:S(2)}) collective-permute-start(bf16[1280,384]{1,0:T(8,128)(2,1)S(1)} %get-tuple-element.30), channel_id=1, source_target_pairs={{0,16},{16,0},{1,17},{17,1},{2,18},{18,2},{3,19},{19,3},{4,20},{20... | collective-permute-start | bytes 2949128 | tf_op jit(solution)/shard_map/ppermute | solution.py:116
  212.8 41.0 %collective-permute-start.4 = (bf16[1280,384]{1,0:T(8,128)(2,1)}, bf16[1280,384]{1,0:T(8,128)(2,1)}, u32[]{:S(2)}, u32[]{:S(2)}) collective-permute-start(bf16[1280,384]{1,0:T(8,128)(2,1)} %get-tuple-element.27), channel_id=1, source_target_pairs={{0,16},{16,0},{1,17},{17,1},{2,18},{18,2},{3,19},{19,3},{4,20},{20... | collective-permute-start | bytes 2949128 | tf_op jit(solution)/shard_map/ppermute | solution.py:116
  215.3 19.6 %copy-start.12 = (f32[768,384]{0,1:T(8,128)S(1)}, f32[768,384]{0,1:T(8,128)}, u32[]{:S(2)}) copy-start(f32[768,384]{0,1:T(8,128)} %fusion.24) | copy-start | bytes 3538948
  256.8 3.2 copy-start.15
  256.8 3.5 copy-start.17
  259.9 1.7 copy-start.2
  261.9 5.2 %copy-start.8 = (bf16[5120,384]{1,0:T(8,128)(2,1)S(1)}, bf16[5120,384]{1,0:T(8,128)(2,1)}, u32[]{:S(2)}) copy-start(bf16[5120,384]{1,0:T(8,128)(2,1)} %all-gather.11.cloned.1.call-done) | copy-start | bytes 11796484
  265.5 65.4 %collective-permute-start.8 = (bf16[1280,384]{1,0:T(8,128)(2,1)}, bf16[1280,384]{1,0:T(8,128)(2,1)}, u32[]{:S(2)}, u32[]{:S(2)}) collective-permute-start(bf16[1280,384]{1,0:T(8,128)(2,1)} %get-tuple-element.23), channel_id=1, source_target_pairs={{0,16},{16,0},{1,17},{17,1},{2,18},{18,2},{3,19},{19,3},{4,20},{20... | collective-permute-start | bytes 2949128 | tf_op jit(solution)/shard_map/ppermute | solution.py:116
  272.7 65.7 %copy-start.4 = (f32[384,768]{1,0:T(8,128)}, f32[384,768]{1,0:T(8,128)S(1)}, u32[]{:S(2)}) copy-start(f32[384,768]{1,0:T(8,128)S(1)} %fusion.96) | copy-start | bytes 3538948
  272.7 63.3 %collective-permute-start.6 = (bf16[1280,384]{1,0:T(8,128)(2,1)}, bf16[1280,384]{1,0:T(8,128)(2,1)}, u32[]{:S(2)}, u32[]{:S(2)}) collective-permute-start(bf16[1280,384]{1,0:T(8,128)(2,1)} %get-tuple-element.22), channel_id=1, source_target_pairs={{0,16},{16,0},{1,17},{17,1},{2,18},{18,2},{3,19},{19,3},{4,20},{20... | collective-permute-start | bytes 2949128 | tf_op jit(solution)/shard_map/ppermute | solution.py:116
  273.3 60.4 %collective-permute-start.7 = (bf16[1280,384]{1,0:T(8,128)(2,1)}, bf16[1280,384]{1,0:T(8,128)(2,1)}, u32[]{:S(2)}, u32[]{:S(2)}) collective-permute-start(bf16[1280,384]{1,0:T(8,128)(2,1)} %get-tuple-element.24), channel_id=1, source_target_pairs={{0,16},{16,0},{1,17},{17,1},{2,18},{18,2},{3,19},{19,3},{4,20},{20... | collective-permute-start | bytes 2949128 | tf_op jit(solution)/shard_map/ppermute | solution.py:116
  317.8 10.6 %copy-start.13 = (bf16[1280,384]{1,0:T(8,128)(2,1)S(1)}, bf16[1280,384]{1,0:T(8,128)(2,1)}, u32[]{:S(2)}) copy-start(bf16[1280,384]{1,0:T(8,128)(2,1)} %get-tuple-element.13) | copy-start | bytes 2949124
  317.8 55.2 %collective-permute-start.10 = (bf16[768,1536]{1,0:T(8,128)(2,1)}, bf16[768,1536]{1,0:T(8,128)(2,1)}, u32[]{:S(2)}, u32[]{:S(2)}) collective-permute-start(bf16[768,1536]{1,0:T(8,128)(2,1)} %pad_maximum_fusion.2), channel_id=1, source_target_pairs={{4,0},{8,4},{12,8},{5,1},{9,5},{13,9},{6,2},{10,6},{14,10},{7,3},{... | collective-permute-start | bytes 7077896 | tf_op jit(solution)/shard_map/ppermute | solution.py:19
  319.2 14.5 %slice-start.2 = ((s8[7864320]{0:T(1024)(128)(4,1)}), s8[4194304]{0:T(1024)(128)(4,1)S(1)}, s32[]{:S(2)}) async-start(s8[7864320]{0:T(1024)(128)(4,1)} %bitcast.52), calls=%async_computation.8 | async-start | bytes 8388608
  322.2 11.6 %slice-start.3 = ((s8[7864320]{0:T(1024)(128)(4,1)}), s8[3670016]{0:T(1024)(128)(4,1)S(1)}, s32[]{:S(2)}) async-start(s8[7864320]{0:T(1024)(128)(4,1)} %bitcast.52), calls=%async_computation.9 | async-start | bytes 7340032
  322.2 55.2 %collective-permute-start.9 = (bf16[768,1536]{1,0:T(8,128)(2,1)}, bf16[768,1536]{1,0:T(8,128)(2,1)}, u32[]{:S(2)}, u32[]{:S(2)}) collective-permute-start(bf16[768,1536]{1,0:T(8,128)(2,1)} %pad_maximum_fusion.2), channel_id=1, source_target_pairs={{0,4},{4,8},{8,12},{1,5},{5,9},{9,13},{2,6},{6,10},{10,14},{3,7},{... | collective-permute-start | bytes 7077896 | tf_op jit(solution)/shard_map/ppermute | solution.py:19
  340.6 2.0 copy-start.18
  374.7 4.4 copy-start.3
  395.0 95.1 %all-gather.17.cloned.1.call-start = ((), (), s32[]{:S(2)}) async-start(), calls=%async_computation.5 | async-start | bytes 3932160 | tf_op jit(solution)/shard_map/all_gather | solution.py:163
  422.6 26.9 %copy-start.5 = (bf16[768,640]{1,0:T(8,128)(2,1)S(1)}, bf16[768,640]{1,0:T(8,128)(2,1)}, u32[]{:S(2)}) copy-start(bf16[768,640]{1,0:T(8,128)(2,1)} %get-tuple-element.18) | copy-start | bytes 2949124
  422.6 24.9 %collective-permute-start.13 = (bf16[768,640]{1,0:T(8,128)(2,1)}, bf16[768,640]{1,0:T(8,128)(2,1)}, u32[]{:S(2)}, u32[]{:S(2)}) collective-permute-start(bf16[768,640]{1,0:T(8,128)(2,1)} %get-tuple-element.20), channel_id=1, source_target_pairs={{0,16},{16,0},{1,17},{17,1},{2,18},{18,2},{3,19},{19,3},{4,20},{20... | collective-permute-start | bytes 2949128 | tf_op jit(solution)/shard_map/ppermute | solution.py:116
  424.1 44.4 %collective-permute-start.11 = (bf16[768,640]{1,0:T(8,128)(2,1)}, bf16[768,640]{1,0:T(8,128)(2,1)S(1)}, u32[]{:S(2)}, u32[]{:S(2)}) collective-permute-start(bf16[768,640]{1,0:T(8,128)(2,1)} %get-tuple-element.21), channel_id=1, source_target_pairs={{0,16},{16,0},{1,17},{17,1},{2,18},{18,2},{3,19},{19,3},{4,20},{20... | collective-permute-start | bytes 2949128 | tf_op jit(solution)/shard_map/ppermute | solution.py:116
  424.7 62.5 %collective-permute-start.12 = (bf16[768,640]{1,0:T(8,128)(2,1)}, bf16[768,640]{1,0:T(8,128)(2,1)S(1)}, u32[]{:S(2)}, u32[]{:S(2)}) collective-permute-start(bf16[768,640]{1,0:T(8,128)(2,1)} %get-tuple-element.19), channel_id=1, source_target_pairs={{0,16},{16,0},{1,17},{17,1},{2,18},{18,2},{3,19},{19,3},{4,20},{20... | collective-permute-start | bytes 2949128 | tf_op jit(solution)/shard_map/ppermute | solution.py:116
  447.6 21.0 %copy-start.11 = (bf16[256,3072]{1,0:T(8,128)(2,1)S(1)}, bf16[256,3072]{1,0:T(8,128)(2,1)}, u32[]{:S(2)}) copy-start(bf16[256,3072]{1,0:T(8,128)(2,1)} %all-gather.15.cloned.1.call-done) | copy-start | bytes 4718596
  468.6 19.1 %copy-start.7 = (bf16[3072,640]{1,0:T(8,128)(2,1)S(1)}, bf16[3072,640]{1,0:T(8,128)(2,1)}, u32[]{:S(2)}) copy-start(bf16[3072,640]{1,0:T(8,128)(2,1)} %all-gather.13.cloned.1.call-done) | copy-start | bytes 11796484
  490.1 5.8 %copy-start.14 = (bf16[512,3072]{1,0:T(8,128)(2,1)S(1)}, bf16[512,3072]{1,0:T(8,128)(2,1)}, u32[]{:S(2)}) copy-start(bf16[512,3072]{1,0:T(8,128)(2,1)} %all-gather.17.cloned.1.call-done) | copy-start | bytes 9437188
  500.4 1.1 copy-start.6
  500.4 2.5 copy-start.1
Sparse Core Ops, SparseCore 0:
  9.1 79.1 all-gather.8
  89.9 74.9 all-gather.6
  166.4 74.9 all-gather.10
  242.8 74.9 all-gather.12
  395.1 21.5 all-gather.14
  419.3 30.3 all-gather.16

commit v3 on v2

--- a/solution.py
+++ b/solution.py
@@ -70,7 +70,7 @@
         o_ref[pl.ds(start, TILE), :] = jnp.where(live, acc, 0.0).astype(o_ref.dtype)
         return carry
 
-    lax.fori_loop(0, tiles, one_tile, 0)
+    lax.fori_loop(0, tiles, one_tile, 0, unroll=True)
 
 
 def attend(query, keys, values, blocks, limits, first_tile=0, interpret=False):
@@ -142,10 +142,10 @@
     values = split_dot(tokens, trade(v_got)).astype(jnp.bfloat16)
     keys, values, q_got = lax.optimization_barrier((keys, values, q_got))
     query = head_norm(split_dot(tokens, trade(q_got)), q_gain)
+    keys, values, o_got = lax.optimization_barrier((keys, values, o_got))
+    o_rows = trade(o_got)
+    both = jnp.concatenate([keys, values], axis=1)
     width = keys.shape[1]
-    both, o_got = lax.optimization_barrier((jnp.concatenate([keys, values], axis=1), o_got))
-    keys, values = both[:, :width], both[:, width:]
-    o_rows = trade(o_got)
     before = shifted(both, "frames", 1)
     after = shifted(both, "frames", -1)
     key_window = jnp.concatenate([before[:, :width], keys, after[:, :width]], axis=0)
@@ -155,7 +155,7 @@
     count_pad = jnp.concatenate([zero, slab_counts, zero], axis=0)
     limits = lax.dynamic_slice_in_dim(count_pad, position, 3, 0)
     tiles = query.shape[0] // TILE
-    half = tiles // 3
+    half = tiles // 2
     mixed = []
     for lo, hi in ((0, half), (half, tiles)):
         part = attend(query[lo * TILE:hi * TILE], key_window, value_window,

time: 511 us -> 504 us (0.986)
  Pallas kernels: 35.1 us -> 28.5 us
    pallas_call x2, Pallas kernels: 35.1 us -> 28.5 us  [attend(): pl.pallas_call(functools.partial(attend_kernel, first_tile=first_tile), g...]
  transfers between devices with their start and end apart: 20 -> 20, of which waited for: 11 -> 10; matrix products, arithmetic and copies ran while one was open for 18% -> 19% of each run, Pallas kernels for 4% -> 3%
where the time goes in v3:
time: 504 us; the launch traced here: 503 us
  waiting for transfers between devices  324 us (64%)
  matrix products  66.6 us (13%)
  local copies, waits for them, and re-layouts  36.9 us (7%)
  Pallas kernels  28.5 us (6%)
  starting transfers between devices  21.8 us (4%)
  between operations  14.1 us (3%)
  other arithmetic  10.9 us (2%)
    all_gather x4, waiting for transfers between devices, fetch(): return (lax.all_gather(mine, 'frames', axis=0, tiled=True), other)  177 us
    ppermute x12, waiting for transfers between devices, trade(): recv.append(lax.ppermute(part, 'clips', [(0, 1), (1, 0)]))  118 us
    ppermute x2, waiting for transfers between devices, shifted(): return lax.ppermute(value, axis, pairs)  29.7 us
    dot_general x15, matrix products, split_dot(): jnp.dot(lax.dynamic_slice_in_dim(x, at * rows, rows, 1), part, preferred_...  29.7 us
    pallas_call x2, Pallas kernels, attend(): pl.pallas_call(functools.partial(attend_kernel, first_tile=first_tile), g...  28.5 us
    dot_general x5, matrix products, split_dot(): own = jnp.dot(x, got, preferred_element_type=jnp.float32)  25.6 us
    ppermute x12, starting transfers between devices, trade(): recv.append(lax.ppermute(part, 'clips', [(0, 1), (1, 0)]))  14.1 us
    dynamic_slice x4, local copies, waits for them, and re-layouts, trade(): part = lax.dynamic_slice_in_dim(got, at * rows, rows, 0)  12.7 us
  transfers between devices with their start and end apart: 20, of which 10 were waited for; matrix products, arithmetic and copies ran while one was open for 19% of the time, Pallas kernels for 3%

profile of v3, /device:TPU:0, one launch (start us, length us, event | category | flops | bytes accessed | tf_op | source)
XLA Modules:
  0.0 503.0 jit_solution(5380589791890655797)
XLA Ops:
  6.5 2.4 constant_dynamic-slice_fusion.13
  9.0 1.1 constant_dynamic-slice_fusion.17
  10.2 3.0 constant_dynamic-slice_fusion.8
  13.2 2.6 constant_dynamic-slice_fusion.3
  16.0 3.7 fusion.25
  19.7 3.9 fusion.23
  24.8 63.4 %all-gather.9.cloned.1.call-done = bf16[5120,384]{1,0:T(8,128)(2,1)} async-done(((bf16[1280,384]{1,0:T(8,128)(2,1)}), bf16[5120,384]{1,0:T(8,128)(2,1)}) %all-gather.9.cloned.1.call-update) | async-done | bytes 3932176 | tf_op jit(solution)/shard_map/all_gather | solution.py:104
  88.3 3.5 constant_dynamic-slice_fusion.12
  91.7 1.5 collective-permute-start.3
  93.8 71.0 %all-gather.7.cloned.1.call-done = bf16[5120,384]{1,0:T(8,128)(2,1)} async-done(((bf16[1280,384]{1,0:T(8,128)(2,1)}), bf16[5120,384]{1,0:T(8,128)(2,1)}) %all-gather.7.cloned.1.call-update) | async-done | bytes 3932176 | tf_op jit(solution)/shard_map/all_gather | solution.py:104
  164.8 2.2 constant_dynamic-slice_fusion.16
  167.1 1.5 collective-permute-start
  169.2 1.5 collective-permute-start.1
  170.6 6.9 %fusion.96 = f32[384,768]{1,0:T(8,128)S(1)} fusion(bf16[5120,384]{1,0:T(8,128)(2,1)S(1)} %copy-done.10, bf16[768,5120]{1,0:T(8,128)(2,1)} %param.9), kind=kOutput, calls=%fused_computation.118 | convolution fusion | flops 3019898880 | bytes 12976128 | tf_op jit(solution)/shard_map/dot_general | solution.py:125
  177.6 5.0 convolution_bitcast_fusion
  182.7 30.2 %collective-permute-done.2 = bf16[1280,384]{1,0:T(8,128)(2,1)S(1)} collective-permute-done((bf16[1280,384]{1,0:T(8,128)(2,1)S(1)}, bf16[1280,384]{1,0:T(8,128)(2,1)S(1)}, u32[]{:S(2)}, u32[]{:S(2)}) %collective-permute-start.2) | collective-permute-done | bytes 983072 | tf_op jit(solution)/shard_map/ppermute | solution.py:116
  212.8 1.5 collective-permute-start.4
  214.3 1.0 fusion.7
  215.3 18.5 %collective-permute-done.1 = bf16[1280,384]{1,0:T(8,128)(2,1)S(1)} collective-permute-done((bf16[1280,384]{1,0:T(8,128)(2,1)S(1)}, bf16[1280,384]{1,0:T(8,128)(2,1)S(1)}, u32[]{:S(2)}, u32[]{:S(2)}) %collective-permute-start.1) | collective-permute-done | bytes 983072 | tf_op jit(solution)/shard_map/ppermute | solution.py:116
  234.9 1.2 fusion.49
  236.6 2.0 copy.23
  238.6 3.0 fusion.5
  241.6 12.2 %collective-permute-done.4 = bf16[1280,384]{1,0:T(8,128)(2,1)} collective-permute-done((bf16[1280,384]{1,0:T(8,128)(2,1)}, bf16[1280,384]{1,0:T(8,128)(2,1)}, u32[]{:S(2)}, u32[]{:S(2)}) %collective-permute-start.4) | collective-permute-done | bytes 983072 | tf_op jit(solution)/shard_map/ppermute | solution.py:116
  253.8 3.0 fusion.11
  256.8 3.1 fusion.52
  260.2 1.4 copy-done.2
  261.8 3.7 constant_dynamic-slice_fusion.7
  265.5 1.5 collective-permute-start.8
  267.6 6.6 %fusion.97 = f32[384,768]{1,0:T(8,128)} fusion(bf16[5120,384]{1,0:T(8,128)(2,1)S(1)} %copy-done.8, bf16[768,5120]{1,0:T(8,128)(2,1)} %param.9), kind=kOutput, calls=%fused_computation.119 | convolution fusion | flops 3019898880 | bytes 12976128 | tf_op jit(solution)/shard_map/dot_general | solution.py:125
  274.2 1.5 collective-permute-start.6
  275.7 42.1 %all-gather.13.cloned.1.call-done = bf16[3072,640]{1,0:T(8,128)(2,1)} async-done(((bf16[768,640]{1,0:T(8,128)(2,1)}), bf16[3072,640]{1,0:T(8,128)(2,1)}) %all-gather.13.cloned.1.call-update) | async-done | bytes 3932176 | tf_op jit(solution)/shard_map/all_gather | solution.py:104
  317.8 1.2 constant_dynamic-update-slice_fusion.1
  318.9 1.1 constant_dynamic-update-slice_fusion
  320.1 1.5 collective-permute-start.10
  321.6 6.0 %collective-permute-start.9 = (bf16[768,1536]{1,0:T(8,128)(2,1)}, bf16[768,1536]{1,0:T(8,128)(2,1)}, u32[]{:S(2)}, u32[]{:S(2)}) collective-permute-start(bf16[768,1536]{1,0:T(8,128)(2,1)} %constant_dynamic-update-slice_fusion), channel_id=1, source_target_pairs={{0,4},{4,8},{8,12},{1,5},{5,9},{9,13},{2,6},{6,10},{10,14},{3,7},{... | collective-permute-start | bytes 7077896 | tf_op jit(solution)/shard_map/ppermute | solution.py:19
  327.6 2.5 fusion.21
  330.2 2.8 fusion.3
  333.0 2.2 fusion.9
  335.3 2.4 fusion.55
  338.0 1.6 fusion.36
  339.6 3.1 copy.29
  342.7 1.8 multiply_convert_fusion
  344.6 1.1 fusion.94
  345.7 29.7 %collective-permute-done.10 = bf16[768,1536]{1,0:T(8,128)(2,1)} collective-permute-done((bf16[768,1536]{1,0:T(8,128)(2,1)}, bf16[768,1536]{1,0:T(8,128)(2,1)}, u32[]{:S(2)}, u32[]{:S(2)}) %collective-permute-start.10) | collective-permute-done | bytes 2359328 | tf_op jit(solution)/shard_map/ppermute | solution.py:19
  375.4 1.8 fusion.93
  377.2 1.8 fusion.92
  378.9 3.3 pad_maximum_fusion
  382.3 14.1 %shard_map.91 = bf16[384,768]{1,0:T(8,128)(2,1)} custom-call(s32[3,8]{1,0:T(4,128)} %get-tuple-element.43.kb_ref, s32[3]{0:T(128)} %dynamic_slice.107.lim_ref, bf16[384,768]{1,0:T(8,128)(2,1)} %get-tuple-element.41.q_ref, bf16[2304,768]{1,0:T(8,128)(2,1)} %get-tuple-element.45.k_ref, bf16[2304,768]{1,0:T(8,128)(2,1)} %get-tuple-element.46.v_ref), custom_call_target="tpu_custom_call" | custom-call | tf_op jit(solution)/shard_map/pallas_call | solution.py:90
  396.5 14.4 %shard_map.92 = bf16[384,768]{1,0:T(8,128)(2,1)} custom-call(s32[3,8]{1,0:T(4,128)} %get-tuple-element.44.kb_ref, s32[3]{0:T(128)} %dynamic_slice.107.lim_ref, bf16[384,768]{1,0:T(8,128)(2,1)} %get-tuple-element.42.q_ref, bf16[2304,768]{1,0:T(8,128)(2,1)} %get-tuple-element.45.k_ref, bf16[2304,768]{1,0:T(8,128)(2,1)} %get-tuple-element.46.v_ref), custom_call_target="tpu_custom_call" | custom-call | tf_op jit(solution)/shard_map/pallas_call | solution.py:90
  410.9 3.3 constant_dynamic-slice_fusion.1
  414.3 1.5 collective-permute-start.13
  416.3 1.5 collective-permute-start.12
  417.8 21.1 %collective-permute-done.13 = bf16[768,640]{1,0:T(8,128)(2,1)S(1)} collective-permute-done((bf16[768,640]{1,0:T(8,128)(2,1)S(1)}, bf16[768,640]{1,0:T(8,128)(2,1)S(1)}, u32[]{:S(2)}, u32[]{:S(2)}) %collective-permute-start.13) | collective-permute-done | bytes 983072 | tf_op jit(solution)/shard_map/ppermute | solution.py:116
  438.9 1.8 fusion.66
  441.4 18.7 %collective-permute-done.11 = bf16[768,640]{1,0:T(8,128)(2,1)} collective-permute-done((bf16[768,640]{1,0:T(8,128)(2,1)}, bf16[768,640]{1,0:T(8,128)(2,1)}, u32[]{:S(2)}, u32[]{:S(2)}) %collective-permute-start.11) | collective-permute-done | bytes 983072 | tf_op jit(solution)/shard_map/ppermute | solution.py:116
  460.1 1.9 convolution_add_fusion.3
  461.9 17.0 %collective-permute-done.12 = bf16[768,640]{1,0:T(8,128)(2,1)} collective-permute-done((bf16[768,640]{1,0:T(8,128)(2,1)}, bf16[768,640]{1,0:T(8,128)(2,1)}, u32[]{:S(2)}, u32[]{:S(2)}) %collective-permute-start.12) | collective-permute-done | bytes 983072 | tf_op jit(solution)/shard_map/ppermute | solution.py:116
  479.0 1.9 fusion.38
  480.9 2.0 fusion.98
  482.9 1.2 fusion.1
  484.1 5.0 fusion.99
  490.3 1.9 convolution_add_fusion.1
  492.2 2.0 fusion.39
  494.4 1.4 pad_maximum_fusion.2
  (90 shorter events, 8.7 us)
Async XLA Ops:
  6.5 2.5 copy-start
  6.5 81.7 %all-gather.9.cloned.1.call-start = ((), (), s32[]{:S(2)}) async-start(), calls=%async_computation.1 | async-start | bytes 4915200 | tf_op jit(solution)/shard_map/all_gather | solution.py:104
  9.0 155.8 %all-gather.7.cloned.1.call-start = ((), (), s32[]{:S(2)}) async-start(), calls=%async_computation | async-start | bytes 4915200 | tf_op jit(solution)/shard_map/all_gather | solution.py:104
  10.1 251.7 %all-gather.11.cloned.1.call-start = ((), (), s32[]{:S(2)}) async-start(), calls=%async_computation.2 | async-start | bytes 4915200 | tf_op jit(solution)/shard_map/all_gather | solution.py:104
  13.2 304.6 %all-gather.13.cloned.1.call-start = ((), (), s32[]{:S(2)}) async-start(), calls=%async_computation.3 | async-start | bytes 4915200 | tf_op jit(solution)/shard_map/all_gather | solution.py:104
  15.9 423.0 %all-gather.15.cloned.1.call-start = ((), (), s32[]{:S(2)}) async-start(), calls=%async_computation.4 | async-start | bytes 2949120 | tf_op jit(solution)/shard_map/all_gather | solution.py:163
  16.0 3.7 copy-start.15
  19.7 3.9 copy-start.16
  19.7 4.5 copy-start.19
  91.7 165.0 %collective-permute-start.3 = (bf16[1280,384]{1,0:T(8,128)(2,1)}, bf16[1280,384]{1,0:T(8,128)(2,1)}, u32[]{:S(2)}, u32[]{:S(2)}) collective-permute-start(bf16[1280,384]{1,0:T(8,128)(2,1)} %get-tuple-element.27), channel_id=1, source_target_pairs={{0,16},{16,0},{1,17},{17,1},{2,18},{18,2},{3,19},{19,3},{4,20},{20... | collective-permute-start | bytes 2949128 | tf_op jit(solution)/shard_map/ppermute | solution.py:116
  93.2 145.4 %collective-permute-start.5 = (bf16[1280,384]{1,0:T(8,128)(2,1)}, bf16[1280,384]{1,0:T(8,128)(2,1)}, u32[]{:S(2)}, u32[]{:S(2)}) collective-permute-start(bf16[1280,384]{1,0:T(8,128)(2,1)} %get-tuple-element.28), channel_id=1, source_target_pairs={{0,16},{16,0},{1,17},{17,1},{2,18},{18,2},{3,19},{19,3},{4,20},{20... | collective-permute-start | bytes 2949128 | tf_op jit(solution)/shard_map/ppermute | solution.py:116
  164.8 5.8 %copy-start.10 = (bf16[5120,384]{1,0:T(8,128)(2,1)S(1)}, bf16[5120,384]{1,0:T(8,128)(2,1)}, u32[]{:S(2)}) copy-start(bf16[5120,384]{1,0:T(8,128)(2,1)} %all-gather.7.cloned.1.call-done) | copy-start | bytes 11796484
  167.1 67.8 %collective-permute-start = (bf16[1280,384]{1,0:T(8,128)(2,1)S(1)}, bf16[1280,384]{1,0:T(8,128)(2,1)S(1)}, u32[]{:S(2)}, u32[]{:S(2)}) collective-permute-start(bf16[1280,384]{1,0:T(8,128)(2,1)S(1)} %get-tuple-element.30), channel_id=1, source_target_pairs={{0,16},{16,0},{1,17},{17,1},{2,18},{18,2},{3,19},{19,3},{4,20},{20... | collective-permute-start | bytes 2949128 | tf_op jit(solution)/shard_map/ppermute | solution.py:116
  168.6 44.2 %collective-permute-start.2 = (bf16[1280,384]{1,0:T(8,128)(2,1)S(1)}, bf16[1280,384]{1,0:T(8,128)(2,1)S(1)}, u32[]{:S(2)}, u32[]{:S(2)}) collective-permute-start(bf16[1280,384]{1,0:T(8,128)(2,1)S(1)} %get-tuple-element.31), channel_id=1, source_target_pairs={{0,16},{16,0},{1,17},{17,1},{2,18},{18,2},{3,19},{19,3},{4,20},{20... | collective-permute-start | bytes 2949128 | tf_op jit(solution)/shard_map/ppermute | solution.py:116
  169.2 8.4 %slice-start = ((s8[7864320]{0:T(1024)(128)(4,1)}), s8[4194304]{0:T(1024)(128)(4,1)S(1)}, s32[]{:S(2)}) async-start(s8[7864320]{0:T(1024)(128)(4,1)} %bitcast.50), calls=%async_computation.6 | async-start | bytes 8388608
  169.2 8.4 %slice-start.1 = ((s8[7864320]{0:T(1024)(128)(4,1)}), s8[3670016]{0:T(1024)(128)(4,1)S(1)}, s32[]{:S(2)}) async-start(s8[7864320]{0:T(1024)(128)(4,1)} %bitcast.50), calls=%async_computation.7 | async-start | bytes 7340032
  169.2 8.5 %copy-start.9 = (bf16[5120,384]{1,0:T(8,128)(2,1)S(1)}, bf16[5120,384]{1,0:T(8,128)(2,1)}, u32[]{:S(2)}) copy-start(bf16[5120,384]{1,0:T(8,128)(2,1)} %all-gather.9.cloned.1.call-done) | copy-start | bytes 11796484
  169.2 64.7 %collective-permute-start.1 = (bf16[1280,384]{1,0:T(8,128)(2,1)S(1)}, bf16[1280,384]{1,0:T(8,128)(2,1)S(1)}, u32[]{:S(2)}, u32[]{:S(2)}) collective-permute-start(bf16[1280,384]{1,0:T(8,128)(2,1)S(1)} %get-tuple-element.32), channel_id=1, source_target_pairs={{0,16},{16,0},{1,17},{17,1},{2,18},{18,2},{3,19},{19,3},{4,20},{20... | collective-permute-start | bytes 2949128 | tf_op jit(solution)/shard_map/ppermute | solution.py:116
  212.8 41.0 %collective-permute-start.4 = (bf16[1280,384]{1,0:T(8,128)(2,1)}, bf16[1280,384]{1,0:T(8,128)(2,1)}, u32[]{:S(2)}, u32[]{:S(2)}) collective-permute-start(bf16[1280,384]{1,0:T(8,128)(2,1)} %get-tuple-element.29), channel_id=1, source_target_pairs={{0,16},{16,0},{1,17},{17,1},{2,18},{18,2},{3,19},{19,3},{4,20},{20... | collective-permute-start | bytes 2949128 | tf_op jit(solution)/shard_map/ppermute | solution.py:116
  215.3 19.6 %copy-start.12 = (f32[768,384]{0,1:T(8,128)S(1)}, f32[768,384]{0,1:T(8,128)}, u32[]{:S(2)}) copy-start(f32[768,384]{0,1:T(8,128)} %fusion.25) | copy-start | bytes 3538948
  241.6 15.2 %copy-start.11 = (f32[768,384]{1,0:T(8,128)S(1)}, f32[768,384]{1,0:T(8,128)}, u32[]{:S(2)}) copy-start(f32[768,384]{1,0:T(8,128)} %fusion.23) | copy-start | bytes 3538948
  256.8 3.1 copy-start.14
  256.8 3.4 copy-start.17
  259.9 1.7 copy-start.2
  261.8 5.7 %copy-start.8 = (bf16[5120,384]{1,0:T(8,128)(2,1)S(1)}, bf16[5120,384]{1,0:T(8,128)(2,1)}, u32[]{:S(2)}) copy-start(bf16[5120,384]{1,0:T(8,128)(2,1)} %all-gather.11.cloned.1.call-done) | copy-start | bytes 11796484
  265.5 64.7 %collective-permute-start.8 = (bf16[1280,384]{1,0:T(8,128)(2,1)}, bf16[1280,384]{1,0:T(8,128)(2,1)}, u32[]{:S(2)}, u32[]{:S(2)}) collective-permute-start(bf16[1280,384]{1,0:T(8,128)(2,1)} %get-tuple-element.25), channel_id=1, source_target_pairs={{0,16},{16,0},{1,17},{17,1},{2,18},{18,2},{3,19},{19,3},{4,20},{20... | collective-permute-start | bytes 2949128 | tf_op jit(solution)/shard_map/ppermute | solution.py:116
  267.0 66.0 %collective-permute-start.7 = (bf16[1280,384]{1,0:T(8,128)(2,1)}, bf16[1280,384]{1,0:T(8,128)(2,1)}, u32[]{:S(2)}, u32[]{:S(2)}) collective-permute-start(bf16[1280,384]{1,0:T(8,128)(2,1)} %get-tuple-element.26), channel_id=1, source_target_pairs={{0,16},{16,0},{1,17},{17,1},{2,18},{18,2},{3,19},{19,3},{4,20},{20... | collective-permute-start | bytes 2949128 | tf_op jit(solution)/shard_map/ppermute | solution.py:116
  274.2 61.1 %collective-permute-start.6 = (bf16[1280,384]{1,0:T(8,128)(2,1)}, bf16[1280,384]{1,0:T(8,128)(2,1)}, u32[]{:S(2)}, u32[]{:S(2)}) collective-permute-start(bf16[1280,384]{1,0:T(8,128)(2,1)} %get-tuple-element.24), channel_id=1, source_target_pairs={{0,16},{16,0},{1,17},{17,1},{2,18},{18,2},{3,19},{19,3},{4,20},{20... | collective-permute-start | bytes 2949128 | tf_op jit(solution)/shard_map/ppermute | solution.py:116
  317.8 9.9 %copy-start.13 = (bf16[1280,384]{1,0:T(8,128)(2,1)S(1)}, bf16[1280,384]{1,0:T(8,128)(2,1)}, u32[]{:S(2)}) copy-start(bf16[1280,384]{1,0:T(8,128)(2,1)} %get-tuple-element.14) | copy-start | bytes 2949124
  317.8 15.2 %slice-start.2 = ((s8[7864320]{0:T(1024)(128)(4,1)}), s8[4194304]{0:T(1024)(128)(4,1)S(1)}, s32[]{:S(2)}) async-start(s8[7864320]{0:T(1024)(128)(4,1)} %bitcast.52), calls=%async_computation.8 | async-start | bytes 8388608
  320.1 12.9 %slice-start.3 = ((s8[7864320]{0:T(1024)(128)(4,1)}), s8[3670016]{0:T(1024)(128)(4,1)S(1)}, s32[]{:S(2)}) async-start(s8[7864320]{0:T(1024)(128)(4,1)} %bitcast.52), calls=%async_computation.9 | async-start | bytes 7340032
  320.1 55.3 %collective-permute-start.10 = (bf16[768,1536]{1,0:T(8,128)(2,1)}, bf16[768,1536]{1,0:T(8,128)(2,1)}, u32[]{:S(2)}, u32[]{:S(2)}) collective-permute-start(bf16[768,1536]{1,0:T(8,128)(2,1)} %constant_dynamic-update-slice_fusion), channel_id=1, source_target_pairs={{4,0},{8,4},{12,8},{5,1},{9,5},{13,9},{6,2},{10,6},{14,10},{7,3},{... | collective-permute-start | bytes 7077896 | tf_op jit(solution)/shard_map/ppermute | solution.py:19
  321.6 55.5 %collective-permute-start.9 = (bf16[768,1536]{1,0:T(8,128)(2,1)}, bf16[768,1536]{1,0:T(8,128)(2,1)}, u32[]{:S(2)}, u32[]{:S(2)}) collective-permute-start(bf16[768,1536]{1,0:T(8,128)(2,1)} %constant_dynamic-update-slice_fusion), channel_id=1, source_target_pairs={{0,4},{4,8},{8,12},{1,5},{5,9},{9,13},{2,6},{6,10},{10,14},{3,7},{... | collective-permute-start | bytes 7077896 | tf_op jit(solution)/shard_map/ppermute | solution.py:19
  335.3 2.4 copy-start.3
  339.6 3.1 copy-start.18
  396.4 87.7 %all-gather.17.cloned.1.call-start = ((), (), s32[]{:S(2)}) async-start(), calls=%async_computation.5 | async-start | bytes 2949120 | tf_op jit(solution)/shard_map/all_gather | solution.py:163
  414.3 24.6 %collective-permute-start.13 = (bf16[768,640]{1,0:T(8,128)(2,1)S(1)}, bf16[768,640]{1,0:T(8,128)(2,1)S(1)}, u32[]{:S(2)}, u32[]{:S(2)}) collective-permute-start(bf16[768,640]{1,0:T(8,128)(2,1)S(1)} %get-tuple-element.22), channel_id=1, source_target_pairs={{0,16},{16,0},{1,17},{17,1},{2,18},{18,2},{3,19},{19,3},{4,20},{20... | collective-permute-start | bytes 2949128 | tf_op jit(solution)/shard_map/ppermute | solution.py:116
  415.7 44.3 %collective-permute-start.11 = (bf16[768,640]{1,0:T(8,128)(2,1)}, bf16[768,640]{1,0:T(8,128)(2,1)}, u32[]{:S(2)}, u32[]{:S(2)}) collective-permute-start(bf16[768,640]{1,0:T(8,128)(2,1)} %get-tuple-element.23), channel_id=1, source_target_pairs={{0,16},{16,0},{1,17},{17,1},{2,18},{18,2},{3,19},{19,3},{4,20},{20... | collective-permute-start | bytes 2949128 | tf_op jit(solution)/shard_map/ppermute | solution.py:116
  416.3 62.7 %collective-permute-start.12 = (bf16[768,640]{1,0:T(8,128)(2,1)}, bf16[768,640]{1,0:T(8,128)(2,1)}, u32[]{:S(2)}, u32[]{:S(2)}) collective-permute-start(bf16[768,640]{1,0:T(8,128)(2,1)} %get-tuple-element.21), channel_id=1, source_target_pairs={{0,16},{16,0},{1,17},{17,1},{2,18},{18,2},{3,19},{19,3},{4,20},{20... | collective-permute-start | bytes 2949128 | tf_op jit(solution)/shard_map/ppermute | solution.py:116
  438.9 1.8 copy-start.6
  461.9 18.9 %copy-start.7 = (bf16[3072,640]{1,0:T(8,128)(2,1)S(1)}, bf16[3072,640]{1,0:T(8,128)(2,1)}, u32[]{:S(2)}) copy-start(bf16[3072,640]{1,0:T(8,128)(2,1)} %all-gather.13.cloned.1.call-done) | copy-start | bytes 11796484
  484.1 5.0 copy-start.5
  492.2 2.2 copy-start.4
  494.2 2.0 copy-start.1
Sparse Core Ops, SparseCore 0:
  9.1 79.1 all-gather.8
  89.8 74.9 all-gather.6
  166.4 74.9 all-gather.10
  242.8 74.9 all-gather.12
  396.5 25.4 all-gather.14
  423.4 23.9 all-gather.16
